TPU v7x, 32 devices: a whole 2x2x4 slice. The times are simulated.
32 devices in a mesh: shot: 8 (over z, y), off: 4 (over x, core).
Axes of the slice: x: 2, y: 2, z: 4, core: 2. Of those that a mesh axis runs over, the one named last changes fastest.
Arguments:
- traces: float32 [8192, 2048], P(('shot', 'off')), may hold values from -6 to 6
- cmp_bin: int32 [8192], P(('shot', 'off')), may hold values from 0 to 255, as said below
- offset_class: int32 [8192], P(('shot', 'off')), may hold values from 0 to 79, as said below
- bin_rank: int32 [256], replicated, may hold values from 0 to 255, as said below
- filter_off: float32 [7], replicated, may hold values from -2.5 to 2.5
- filter_time: float32 [65], replicated, may hold values from -2 to 2
Outputs:
- planes: float32 [80, 2048, 256], P('off', 'shot')
Inputs may be any that keep to these rules, and one draw needn't show every extreme that they name: `cmp_bin`: in each aligned block of 256 rows (the rows of one device) at most 128 rows name bins with the same owner bin_rank // 32; one owner, the same for all blocks, gets exactly 128 rows of every block, and every other owner gets a whole number of rows next to 128 / (7) (its floor or ceiling). `offset_class`: row r has a class from g * 20 to g * 20 + 19, with g = (r // 256) % 4. `bin_rank`: A permutation.
All inputs are finite; a program needn't handle non-finite values.
Results may differ from a plain program's by a relative error of at most 0.00007.
Values sent between devices are 32-bit elements; how exact they have to be, the bound alone decides.
No kernel may reach another device: no remote copies, remote signals or barrier semaphores. Data moves between devices by JAX's collectives and lax.ppermute only.
A program may use at most 128 MiB of HBM per device.

v0:
```python
import jax
import jax.numpy as jnp
from jax import lax
from jax.sharding import PartitionSpec as P

OFFC = 80
BOWN = 32


def extended_2(cells, sides, width):
    for axis, dim in sides:
        count = lax.axis_size(axis)
        ends = count - 1
        head = lax.slice_in_dim(cells, 0, width, axis=dim)
        tail = lax.slice_in_dim(cells, cells.shape[dim] - width, cells.shape[dim], axis=dim)
        cells = jnp.concatenate(
            [
                lax.ppermute(tail, axis, [(i, (i + 1) % count) for i in range(ends)]),
                cells,
                lax.ppermute(head, axis, [((i + 1) % count, i) for i in range(ends)]),
            ],
            axis=dim,
        )
    return cells


def tap_table(filter_time, width_in, width_out):
    inner = jnp.arange(width_in, dtype=jnp.int32)[:, None]
    outer = jnp.arange(width_out, dtype=jnp.int32)[None, :]
    distance = inner - outer
    taps = jnp.arange(filter_time.shape[0], dtype=jnp.int32)
    matches = distance[:, :, None] == taps[None, None, :]
    return jnp.sum(jnp.where(matches, filter_time[None, None, :], 0.0), axis=2)


def block_filter(data, filter_time):
    reach = filter_time.shape[0] // 2
    block_width = 128
    leading = data.shape[:-1]
    samples = data.shape[-1]
    blocks = data.reshape(leading + (samples // block_width, block_width))
    zeroes = jnp.zeros(leading + (1, reach), jnp.float32)
    before = jnp.concatenate([zeroes, blocks[..., :-1, block_width - reach :]], axis=-2)
    after = jnp.concatenate([blocks[..., 1:, :reach], zeroes], axis=-2)
    extended = jnp.concatenate([before, blocks, after], axis=-1)
    table = tap_table(filter_time, block_width + 2 * reach, block_width)
    result = jnp.einsum("...ki,io->...ko", extended, table, precision=lax.Precision.HIGHEST)
    return result.reshape(leading + (samples,))


def offset_mix(scaled, filter_off):
    reach = filter_off.shape[0] // 2
    padded = extended_2(scaled, (("off", 0),), reach)
    count = scaled.shape[0]
    mixed = filter_off[0] * padded[0:count]
    for offset_tap in range(1, filter_off.shape[0]):
        mixed = mixed + filter_off[offset_tap] * padded[offset_tap : offset_tap + count]
    return mixed


def stack_cells(received, labels, segments):
    stacked = jax.ops.segment_sum(received, labels, num_segments=segments + 1)[:segments]
    fold_count = jax.ops.segment_sum(
        jnp.ones(labels.shape, jnp.float32), labels, num_segments=segments + 1
    )[:segments]
    return stacked / jnp.maximum(fold_count, 1.0)[:, None]


def body(traces, cmp_bin, offset_class, bin_rank, filter_off, filter_time):
    shots = lax.axis_size("shot")
    off_dev = OFFC // lax.axis_size("off")
    first_class = lax.axis_index("off") * off_dev
    bin_count = bin_rank.shape[0]
    tr_dev = traces.shape[0]
    samples = traces.shape[1]
    matches = cmp_bin[:, None] == jnp.arange(bin_count, dtype=jnp.int32)[None, :]
    rank_of = jnp.sum(jnp.where(matches, bin_rank[None, :], 0), axis=1)
    local_class = offset_class - first_class
    capacity = max(2, 4 * tr_dev // shots)
    owning = rank_of // BOWN
    member = (owning[:, None] == jnp.arange(shots, dtype=jnp.int32)[None, :]).astype(jnp.int32)
    position = jnp.sum(jnp.cumsum(member, axis=0) * member, axis=1) - 1
    target = owning * capacity + position
    sentinel = off_dev * BOWN
    cell_index = local_class * BOWN + rank_of % BOWN
    outgoing = jnp.zeros((shots * capacity, samples), jnp.float32).at[target].set(traces)
    labels = jnp.full((shots * capacity,), sentinel, jnp.int32).at[target].set(cell_index)
    received, arrived = (
        lax.all_to_all(outgoing, "shot", split_axis=0, concat_axis=0, tiled=True),
        lax.all_to_all(labels, "shot", split_axis=0, concat_axis=0, tiled=True),
    )
    scaled = stack_cells(received, arrived, sentinel).reshape(off_dev, BOWN, samples)
    mixed = offset_mix(scaled, filter_off)
    filtered = block_filter(mixed, filter_time)
    relayed = lax.all_to_all(filtered, "shot", split_axis=2, concat_axis=1, tiled=True)
    return jnp.transpose(relayed, (0, 2, 1))


def solution(mesh):
    return jax.shard_map(
        body,
        mesh=mesh,
        in_specs=(P(("shot", "off"), None), P(("shot", "off")), P(("shot", "off")), P(), P(), P()),
        out_specs=P("off", "shot", None),
        check_vma=False,
    )
```

profile of v0, /device:TPU:1, one launch (start us, length us, event | category | flops | bytes accessed | tf_op | source)
XLA Modules:
  0.0 474.8 jit_solution(17869726358721929491)
XLA Ops:
  0.0 0.9 select_reduce_fusion.1
  0.9 0.6 reduce-window.6
  1.5 0.2 slice_reduce_fusion
  1.7 0.7 fusion.34
  2.4 0.1 fusion.28
  2.6 2.0 scatter_custom_fusion
  4.5 6.4 %all-to-all-start = ((s32[8,128,1]{1,2,0:T(1,128)}), s32[8,128,1]{1,2,0:T(1,128)S(1)}, u32[]{:S(2)}, u32[]{:S(2)}) async-start(s32[8,128,1]{1,2,0:T(1,128)} %bitcast.8), calls=%async_computation | async-start | bytes 8192 | tf_op jit(solution)/shard_map/all_to_all | solution.py:90
  10.9 6.6 %scatter_custom_fusion.1 = f32[1024,2048]{1,0:T(8,128)} fusion(s32[256]{0:T(256)S(1)} %bitcast.67, f32[256,2048]{1,0:T(8,128)} %param.6, f32[]{:T(128)} %constant.24.clone.1), kind=kCustom, calls=%fused_computation.44 | custom fusion | bytes 8389120 | tf_op jit(solution)/shard_map/scatter | solution.py:86
  17.5 0.0 all-to-all-done
  17.5 5.4 %all-to-all-start.1 = ((f32[8,128,2048]{2,1,0:T(8,128)}), f32[8,128,2048]{2,1,0:T(8,128)}, u32[]{:S(2)}, u32[]{:S(2)}) async-start(f32[8,128,2048]{2,1,0:T(8,128)} %bitcast.56), calls=%async_computation.1 | async-start | bytes 16777216 | tf_op jit(solution)/shard_map/all_to_all | solution.py:89
  22.9 7.8 %scatter_custom_fusion.3 = f32[641]{0:T(1024)S(1)} fusion(s32[1024]{0:T(1024)S(1)} %bitcast.64, f32[1024]{0:T(1024)S(1)} %broadcast.160, f32[]{:T(128)} %constant.24.clone.1), kind=kCustom, calls=%fused_computation.64 | custom fusion | flops 1024 | bytes 2568 | tf_op jit(solution)/shard_map/scatter-add | solution.py:63
  30.8 173.9 %all-to-all-done.1 = f32[8,128,2048]{2,1,0:T(8,128)} async-done(((f32[8,128,2048]{2,1,0:T(8,128)}), f32[8,128,2048]{2,1,0:T(8,128)}, u32[]{:S(2)}, u32[]{:S(2)}) %all-to-all-start.1) | async-done | bytes 8388640 | tf_op jit(solution)/shard_map/all_to_all | solution.py:89
  204.7 17.4 %scatter_custom_fusion.2 = f32[641,2048]{1,0:T(8,128)} fusion(s32[1024]{0:T(1024)S(1)} %bitcast.65, f32[1024,2048]{1,0:T(8,128)} %bitcast.11, f32[]{:T(128)} %constant.24.clone.1), kind=kCustom, calls=%fused_computation.46 | custom fusion | flops 2097152 | bytes 5251584 | tf_op jit(solution)/shard_map/scatter-add | solution.py:62
  222.0 0.0 copy-start
  222.1 0.0 copy-start.1
  222.1 3.3 slice_divide_fusion
  225.3 0.1 fusion.40
  225.5 5.4 %collective-permute-start = (f32[3,32,2048]{2,1,0:T(8,128)S(1)}, f32[3,32,2048]{2,1,0:T(8,128)S(1)}, u32[]{:S(2)}, u32[]{:S(2)}) collective-permute-start(f32[3,32,2048]{2,1,0:T(8,128)S(1)} %bitcast.61), channel_id=1, source_target_pairs={{0,1},{1,2},{2,3},{4,5},{5,6},{6,7},{8,9},{9,10},{10,11},{12,13},{... | collective-permute-start | bytes 2359304 | tf_op jit(solution)/shard_map/ppermute | solution.py:18
  230.9 2.1 collective-permute-start.1
  233.0 0.0 copy-done
  233.0 0.7 fusion.41
  233.7 0.0 copy-done.1
  233.7 0.8 select_reduce_fusion
  234.5 5.3 %collective-permute-done = f32[3,32,2048]{2,1,0:T(8,128)S(1)} collective-permute-done((f32[3,32,2048]{2,1,0:T(8,128)S(1)}, f32[3,32,2048]{2,1,0:T(8,128)S(1)}, u32[]{:S(2)}, u32[]{:S(2)}) %collective-permute-start) | collective-permute-done | bytes 786464 | tf_op jit(solution)/shard_map/ppermute | solution.py:18
  239.8 4.4 collective-permute-done.1
  244.2 8.8 %fusion.7 = f32[20,32,2048]{2,1,0:T(8,128)S(1)} fusion(f32[20,32,2048]{2,1,0:T(8,128)S(1)} %bitcast.57, f32[3,32,2048]{2,1,0:T(8,128)S(1)} %collective-permute-done.1, f32[3,32,2048]{2,1,0:T(8,128)S(1)} %collective-permute-done, f32[]{:T(128)} %bitcast.20, f32[]{:T(128)} %bitcast.19, f32[]{:T(128)} %bitcast.17, f32[]{:T(128)} %bitcast.16, f32[]{:T(128)} %bitcast.15, ...), kind=kLoop, calls=%fused_computation.25 | loop fusion | flops 24903680 | bytes 12058652 | tf_op jit(solution)/shard_map/add | solution.py:57
  253.0 1.2 copy.25
  254.2 4.2 fusion.39
  258.4 13.8 %fusion = f32[20,32,16,128]{3,2,1,0:T(8,128)} fusion(f32[20,32,15,32]{3,2,1,0:T(8,128)} %get-tuple-element.6, f32[20,32,15,32]{3,2,1,0:T(8,128)S(1)} %get-tuple-element.5, f32[20,32,16,128]{3,2,1,0:T(8,128)S(1)} %bitcast.55, f32[192,128]{1,0:T(8,128)S(1)} %select_reduce_fusion), kind=kOutput, calls=%fused_computation.5 | convolution fusion | flops 3031695360 | bytes 13041664 | tf_op jit(solution)/shard_map/...ki,io->...ko/dot_general | solution.py:47
  272.3 13.1 %copy.22 = f32[20,32,16,128]{1,0,3,2:T(8,128)} copy(f32[20,32,16,128]{3,2,1,0:T(8,128)} %fusion) | data formatting | bytes 10485760 | tf_op jit(solution)/shard_map/reshape | solution.py:48
  285.4 16.2 %reshape.172 = f32[8,1,163840]{2,1,0:T(1,128)} reshape(f32[2048,20,32]{2,1,0:T(8,128)} %bitcast.52) | data formatting | bytes 10485760
  301.6 111.8 %all_to_all.39 = f32[8,1,163840]{2,1,0:T(1,128)} all-to-all(f32[8,1,163840]{2,1,0:T(1,128)} %reshape.172), channel_id=1, replica_groups=mesh['shot'=8,'off'=4] {'shot'}, dimensions={0} | all-to-all | bytes 10485760 | tf_op jit(solution)/shard_map/all_to_all | solution.py:95
  413.3 0.5 broadcast.208
  413.9 16.9 %reduce.2 = f32[8,163840]{1,0:T(8,128)} reduce(f32[8,1,163840]{2,1,0:T(1,128)} %all_to_all.39, f32[]{:T(128)} %broadcast.208), dimensions={1}, to_apply=%all_to_all.32.reduce_sub_computation | reduce | bytes 10485764 | tf_op jit(solution)/shard_map/all_to_all | solution.py:95
  430.7 21.3 %reshape.173 = f32[2048,20,32]{2,1,0:T(8,128)} reshape(f32[8,163840]{1,0:T(8,128)} %reduce.2) | data formatting | bytes 10485760
  452.1 16.4 %copy.19 = f32[20,8,32,256]{3,2,1,0:T(8,128)} copy(f32[20,8,32,256]{2,0,3,1:T(8,128)} %bitcast.53) | data formatting | bytes 10485760 | tf_op jit(solution)/shard_map/all_to_all | solution.py:95
  468.4 5.9 %copy.20 = f32[20,256,256]{2,1,0:T(8,128)} copy(f32[20,256,256]{1,2,0:T(8,128)} %bitcast.59) | data formatting | bytes 10485760 | tf_op jit(solution)/shard_map/transpose | solution.py:96
  (9 shorter events, 0.1 us)
Async XLA Ops:
  4.5 13.0 %all-to-all-start = ((s32[8,128,1]{1,2,0:T(1,128)}), s32[8,128,1]{1,2,0:T(1,128)S(1)}, u32[]{:S(2)}, u32[]{:S(2)}) async-start(s32[8,128,1]{1,2,0:T(1,128)} %bitcast.8), calls=%async_computation | async-start | bytes 8192 | tf_op jit(solution)/shard_map/all_to_all | solution.py:90
  17.5 187.2 %all-to-all-start.1 = ((f32[8,128,2048]{2,1,0:T(8,128)}), f32[8,128,2048]{2,1,0:T(8,128)}, u32[]{:S(2)}, u32[]{:S(2)}) async-start(f32[8,128,2048]{2,1,0:T(8,128)} %bitcast.56), calls=%async_computation.1 | async-start | bytes 16777216 | tf_op jit(solution)/shard_map/all_to_all | solution.py:89
  222.0 11.0 %copy-start = (f32[7]{0:T(128)S(1)}, f32[7]{0:T(128)}, u32[]{:S(2)}) copy-start(f32[7]{0:T(128)} %param.10) | copy-start | bytes 88
  222.1 11.7 %copy-start.1 = (f32[65]{0:T(128)S(1)}, f32[65]{0:T(128)}, u32[]{:S(2)}) copy-start(f32[65]{0:T(128)} %param.11) | copy-start | bytes 784
  225.5 14.3 %collective-permute-start = (f32[3,32,2048]{2,1,0:T(8,128)S(1)}, f32[3,32,2048]{2,1,0:T(8,128)S(1)}, u32[]{:S(2)}, u32[]{:S(2)}) collective-permute-start(f32[3,32,2048]{2,1,0:T(8,128)S(1)} %bitcast.61), channel_id=1, source_target_pairs={{0,1},{1,2},{2,3},{4,5},{5,6},{6,7},{8,9},{9,10},{10,11},{12,13},{... | collective-permute-start | bytes 2359304 | tf_op jit(solution)/shard_map/ppermute | solution.py:18
  230.9 13.3 %collective-permute-start.1 = (f32[3,32,2048]{2,1,0:T(8,128)S(1)}, f32[3,32,2048]{2,1,0:T(8,128)S(1)}, u32[]{:S(2)}, u32[]{:S(2)}) collective-permute-start(f32[3,32,2048]{2,1,0:T(8,128)S(1)} %bitcast.60), channel_id=1, source_target_pairs={{1,0},{2,1},{3,2},{5,4},{6,5},{7,6},{9,8},{10,9},{11,10},{13,12},{... | collective-permute-start | bytes 2359304 | tf_op jit(solution)/shard_map/ppermute | solution.py:20
where the time goes:
time: 480 us; the launch traced here: 475 us
  waiting for transfers between devices  184 us (38%)
  blocking collectives  112 us (23%)
  local copies, waits for them, and re-layouts  88.5 us (18%)
  other arithmetic  57.2 us (12%)
  starting transfers between devices  19.4 us (4%)
  matrix products  13.8 us (3%)
    all_to_all x1, waiting for transfers between devices, body(): lax.all_to_all(outgoing, 'shot', split_axis=0, concat_axis=0, tiled=True)  174 us
    all_to_all x1, blocking collectives, body(): lax.all_to_all(filtered, 'shot', split_axis=2, concat_axis=1, tiled=True)  112 us
    unnamed x7, local copies, waits for them, and re-layouts  38.7 us
    scatter-add x1, other arithmetic, stack_cells(): jax.ops.segment_sum(received, labels, num_segments=segments + 1)[:segments]  17.4 us
    all_to_all x2, local copies, waits for them, and re-layouts, body(): lax.all_to_all(filtered, 'shot', split_axis=2, concat_axis=1, tiled=True)  16.9 us
    all_to_all x1, other arithmetic, body(): lax.all_to_all(filtered, 'shot', split_axis=2, concat_axis=1, tiled=True)  16.9 us
    dot_general x1, matrix products, block_filter(): jnp.einsum('...ki,io->...ko', extended, table, precision=lax.Precision.HI...  13.8 us
    reshape x1, local copies, waits for them, and re-layouts, block_filter(): return result.reshape(leading + (samples,))  13.1 us
  transfers between devices with their start and end apart: 4, of which 3 were waited for; matrix products, arithmetic and copies ran while one was open for 3% of the time, Pallas kernels for 0%

commit v1 on v0

v1 whole, which is shorter than its diff:
```python
import jax
import jax.numpy as jnp
from jax import lax
from jax.sharding import PartitionSpec as P

OFFC = 80


def tap_table(filter_time, width_in, width_out):
    inner = jnp.arange(width_in, dtype=jnp.int32)[:, None]
    outer = jnp.arange(width_out, dtype=jnp.int32)[None, :]
    distance = inner - outer
    taps = jnp.arange(filter_time.shape[0], dtype=jnp.int32)
    matches = distance[:, :, None] == taps[None, None, :]
    return jnp.sum(jnp.where(matches, filter_time[None, None, :], 0.0), axis=2)


def block_filter(data, filter_time):
    reach = filter_time.shape[0] // 2
    block_width = 128
    leading = data.shape[:-1]
    samples = data.shape[-1]
    blocks = data.reshape(leading + (samples // block_width, block_width))
    zeroes = jnp.zeros(leading + (1, reach), jnp.float32)
    before = jnp.concatenate([zeroes, blocks[..., :-1, block_width - reach :]], axis=-2)
    after = jnp.concatenate([blocks[..., 1:, :reach], zeroes], axis=-2)
    extended = jnp.concatenate([before, blocks, after], axis=-1)
    table = tap_table(filter_time, block_width + 2 * reach, block_width)
    result = jnp.einsum("...ki,io->...ko", extended, table, precision=lax.Precision.HIGHEST)
    return result.reshape(leading + (samples,))


def class_halo(cells, reach):
    count = lax.axis_size("off")
    ends = count - 1
    head = cells[:reach]
    tail = cells[cells.shape[0] - reach :]
    before = lax.ppermute(tail, "off", [(i, i + 1) for i in range(ends)])
    after = lax.ppermute(head, "off", [(i + 1, i) for i in range(ends)])
    return jnp.concatenate([before, cells, after], axis=0)


def body(traces, cmp_bin, offset_class, bin_rank, filter_off, filter_time):
    shots = lax.axis_size("shot")
    off_dev = OFFC // lax.axis_size("off")
    first_class = lax.axis_index("off") * off_dev
    bin_count = bin_rank.shape[0]
    tr_dev, samples = traces.shape
    window = samples // shots
    cell_count = off_dev * bin_count

    filtered = block_filter(traces, filter_time)
    outgoing = jnp.transpose(filtered.reshape(tr_dev, shots, window), (1, 0, 2))
    received = lax.all_to_all(outgoing, "shot", 0, 0, tiled=True)
    received = received.reshape(shots * tr_dev, window)

    place = jnp.take(bin_rank, cmp_bin, axis=0)
    cell = (offset_class - first_class) * bin_count + place
    cells = lax.all_gather(cell, "shot", axis=0, tiled=True)

    fold = jax.ops.segment_sum(jnp.ones(cells.shape, jnp.float32), cells, num_segments=cell_count)
    scale = 1.0 / jnp.maximum(jnp.take(fold, cells, axis=0), 1.0)
    stacked = jax.ops.segment_sum(received * scale[:, None], cells, num_segments=cell_count)
    stacked = stacked.reshape(off_dev, bin_count, window)

    reach = filter_off.shape[0] // 2
    padded = class_halo(stacked, reach)
    mixed = filter_off[0] * padded[0:off_dev]
    for offset_tap in range(1, filter_off.shape[0]):
        mixed = mixed + filter_off[offset_tap] * padded[offset_tap : offset_tap + off_dev]
    return jnp.transpose(mixed, (0, 2, 1))


def solution(mesh):
    return jax.shard_map(
        body,
        mesh=mesh,
        in_specs=(P(("shot", "off"), None), P(("shot", "off")), P(("shot", "off")), P(), P(), P()),
        out_specs=P("off", "shot", None),
        check_vma=False,
    )
```

time: 480 us -> 153 us (0.32)
  the two profiles are of different devices: /device:TPU:1 before, /device:TPU:10 now
where the time goes in v1:
time: 153 us
  blocking collectives  53.8 us (35%)
  other arithmetic  47.8 us (31%)
  local copies, waits for them, and re-layouts  26.7 us (17%)
  starting transfers between devices  10.7 us (7%)
  waiting for transfers between devices  10.2 us (7%)
  matrix products  3.56 us (2%)
    all_gather x1, blocking collectives, body(): cells = lax.all_gather(cell, 'shot', axis=0, tiled=True)  53.8 us
    transpose x1, other arithmetic, body(): return jnp.transpose(mixed, (0, 2, 1))  19.5 us
    scatter-add x1, other arithmetic, body(): jax.ops.segment_sum(received * scale[:, None], cells, num_segments=cell_c...  14.6 us
    gather x1, local copies, waits for them, and re-layouts, body(): scale = 1.0 / jnp.maximum(jnp.take(fold, cells, axis=0), 1.0)  11.8 us
    scatter-add x1, other arithmetic, body(): jax.ops.segment_sum(jnp.ones(cells.shape, jnp.float32), cells, num_segmen...  11.2 us
    ppermute x1, waiting for transfers between devices, class_halo(): after = lax.ppermute(head, 'off', [(i + 1, i) for i in range(ends)])  6.34 us
    all_to_all x1, starting transfers between devices, body(): received = lax.all_to_all(outgoing, 'shot', 0, 0, tiled=True)  6.28 us
    transpose x1, local copies, waits for them, and re-layouts, body(): return jnp.transpose(mixed, (0, 2, 1))  5.88 us
  transfers between devices with their start and end apart: 3, of which 2 were waited for; matrix products, arithmetic and copies ran while one was open for 17% of the time, Pallas kernels for 0%

profile of v1, /device:TPU:10, one launch (start us, length us, event | category | flops | bytes accessed | tf_op | source)
XLA Modules:
  0.0 152.9 jit_solution(11362488880727962242)
XLA Ops:
  0.0 0.0 copy-start
  0.0 0.0 copy-start.4
  0.0 1.9 %copy.14 = f32[256,2048]{0,1:T(8,128)S(1)} copy(f32[256,2048]{1,0:T(8,128)} %param.6) | data formatting | bytes 4194304 | tf_op args[0]
  2.0 0.1 fusion.36
  2.1 0.0 copy-done.4
  2.1 0.8 select_reduce_fusion
  2.8 3.6 %fusion.17 = f32[256,16,128]{0,2,1:T(8,128)} fusion(f32[256,15,32]{0,2,1:T(8,128)S(1)} %get-tuple-element.8, f32[256,15,32]{0,2,1:T(8,128)S(1)} %get-tuple-element.7, f32[256,16,128]{0,2,1:T(8,128)S(1)} %bitcast.25, f32[192,128]{1,0:T(8,128)S(1)} %select_reduce_fusion), kind=kOutput, calls=%fused_computation.34 | convolution fusion | flops 1212678144 | bytes 5275648 | tf_op jit(solution)/shard_map/...ki,io->...ko/dot_general | solution.py:29
  6.4 0.0 copy-start.2
  6.4 0.0 copy-start.3
  6.4 2.9 %copy.15 = f32[256,8,256]{2,0,1:T(8,128)} copy(f32[256,8,256]{0,2,1:T(8,128)} %bitcast.26) | data formatting | bytes 4194304 | tf_op jit(solution)/shard_map/reshape;reshape | solution.py:53
  9.3 6.3 %all-to-all-start = ((f32[8,256,256]{2,1,0:T(8,128)}), f32[8,256,256]{2,1,0:T(8,128)S(1)}, u32[]{:S(2)}, u32[]{:S(2)}) async-start(f32[8,256,256]{2,1,0:T(8,128)} %bitcast.23), calls=%async_computation | async-start | bytes 4194304 | tf_op jit(solution)/shard_map/all_to_all | solution.py:54
  15.6 0.0 copy-done.2
  15.6 0.0 copy-done
  15.6 1.9 %gather_fusion = s32[256]{0:T(256)S(1)} fusion(s32[256]{0:T(256)S(1)} %copy-done, s32[1024]{0:T(1024)S(1)} %pad_clamp_fusion), kind=kCustom, calls=%fused_computation | custom fusion | bytes 3072 | tf_op jit(solution)/shard_map/jit(_take)/gather | solution.py:57
  17.6 0.0 copy-done.3
  17.6 53.8 %all-gather = s32[8,1,256]{2,1,0:T(1,128)S(1)} all-gather(s32[1,1,256]{2,1,0:T(1,128)S(1)} %bitcast.33), channel_id=1, replica_groups=mesh['shot'=8,'off'=4] {'shot'}, dimensions={0}, use_global_device_ids=true | all-gather | bytes 9216 | tf_op jit(solution)/shard_map/all_gather | solution.py:59
  71.4 11.2 %scatter_custom_fusion = f32[5120]{0:T(1024)S(1)} fusion(s32[2048]{0:T(1024)S(1)} %bitcast.29, f32[2048]{0:T(1024)S(1)} %broadcast.24, f32[]{:T(128)} %constant.13.clone.1), kind=kCustom, calls=%fused_computation.50 | custom fusion | flops 2048 | bytes 20484 | tf_op jit(solution)/shard_map/scatter-add | solution.py:61
  82.7 11.8 %gather_fusion.1 = f32[2048]{0:T(1024)S(1)} fusion(f32[5120]{0:T(1024)S(1)} %scatter_custom_fusion, s32[2048]{0:T(1024)S(1)} %fusion.29), kind=kCustom, calls=%fused_computation.1 | custom fusion | bytes 24576 | tf_op jit(solution)/shard_map/jit(_take)/gather | solution.py:62
  94.5 0.0 all-to-all-done
  94.5 1.7 %bitcast_multiply_fusion = f32[2048,256]{1,0:T(8,128)} fusion(f32[8,256,256]{2,1,0:T(8,128)S(1)} %all-to-all-done, f32[2048]{0:T(1024)S(1)} %maximum_divide_fusion), kind=kLoop, calls=%fused_computation.43 | loop fusion | flops 524288 | bytes 4202496 | tf_op jit(solution)/shard_map/mul | solution.py:63
  96.2 0.0 copy-start.1
  96.2 14.6 %scatter_custom_fusion.1 = f32[5120,256]{1,0:T(8,128)} fusion(s32[2048]{0:T(1024)S(1)} %bitcast.32, f32[2048,256]{1,0:T(8,128)} %bitcast_multiply_fusion, f32[]{:T(128)} %constant.13.clone.1), kind=kCustom, calls=%fused_computation.41 | custom fusion | flops 524288 | bytes 5243392 | tf_op jit(solution)/shard_map/scatter-add | solution.py:63
  110.8 1.5 fusion.35
  112.3 1.9 %collective-permute-start.1 = (f32[3,256,256]{2,1,0:T(8,128)S(1)}, f32[3,256,256]{2,1,0:T(8,128)S(1)}, u32[]{:S(2)}, u32[]{:S(2)}) collective-permute-start(f32[3,256,256]{2,1,0:T(8,128)S(1)} %bitcast.28), channel_id=1, source_target_pairs={{1,0},{2,1},{3,2},{5,4},{6,5},{7,6},{9,8},{10,9},{11,10},{13,12},{... | collective-permute-start | bytes 2359304 | tf_op jit(solution)/shard_map/ppermute | solution.py:39
  114.2 2.5 %collective-permute-start = (f32[3,256,256]{2,1,0:T(8,128)S(1)}, f32[3,256,256]{2,1,0:T(8,128)S(1)}, u32[]{:S(2)}, u32[]{:S(2)}) collective-permute-start(f32[3,256,256]{2,1,0:T(8,128)S(1)} %bitcast.27), channel_id=1, source_target_pairs={{0,1},{1,2},{2,3},{4,5},{5,6},{6,7},{8,9},{9,10},{10,11},{12,13},{... | collective-permute-start | bytes 2359304 | tf_op jit(solution)/shard_map/ppermute | solution.py:38
  116.7 0.0 copy-done.1
  116.7 0.7 fusion.37
  117.3 6.3 %collective-permute-done.1 = f32[3,256,256]{2,1,0:T(8,128)S(1)} collective-permute-done((f32[3,256,256]{2,1,0:T(8,128)S(1)}, f32[3,256,256]{2,1,0:T(8,128)S(1)}, u32[]{:S(2)}, u32[]{:S(2)}) %collective-permute-start.1) | collective-permute-done | bytes 786464 | tf_op jit(solution)/shard_map/ppermute | solution.py:39
  123.7 3.8 %collective-permute-done = f32[3,256,256]{2,1,0:T(8,128)S(1)} collective-permute-done((f32[3,256,256]{2,1,0:T(8,128)S(1)}, f32[3,256,256]{2,1,0:T(8,128)S(1)}, u32[]{:S(2)}, u32[]{:S(2)}) %collective-permute-start) | collective-permute-done | bytes 786464 | tf_op jit(solution)/shard_map/ppermute | solution.py:38
  127.5 19.5 %fusion.4 = f32[20,256,256]{1,2,0:T(8,128)} fusion(f32[20,256,256]{2,1,0:T(8,128)} %bitcast.22, f32[3,256,256]{2,1,0:T(8,128)S(1)} %collective-permute-done.1, f32[3,256,256]{2,1,0:T(8,128)S(1)} %collective-permute-done, f32[]{:T(128)} %bitcast.16, f32[]{:T(128)} %bitcast.15, f32[]{:T(128)} %bitcast.13, f32[]{:T(128)} %bitcast.12, f32[]{:T(128)} %bitcast.11, ...), kind=kLoop, calls=%fused_computation.18 | loop fusion | flops 24903680 | bytes 12058652 | tf_op jit(solution)/shard_map/transpose | solution.py:71
  147.0 5.9 %copy.16 = f32[20,256,256]{2,1,0:T(8,128)} copy(f32[20,256,256]{1,2,0:T(8,128)} %fusion.4) | data formatting | bytes 10485760 | tf_op jit(solution)/shard_map/transpose | solution.py:71
  (7 shorter events, 0.0 us)
Async XLA Ops:
  0.0 15.6 %copy-start = (s32[256]{0:T(256)S(1)}, s32[256]{0:T(256)}, u32[]{:S(2)}) copy-start(s32[256]{0:T(256)} %param.9) | copy-start | bytes 3076
  0.0 2.1 %copy-start.4 = (f32[65]{0:T(128)S(1)}, f32[65]{0:T(128)}, u32[]{:S(2)}) copy-start(f32[65]{0:T(128)} %param.11) | copy-start | bytes 784
  6.4 9.2 %copy-start.2 = (s32[256]{0:T(256)S(1)}, s32[256]{0:T(256)}, u32[]{:S(2)}) copy-start(s32[256]{0:T(256)} %param.7) | copy-start | bytes 3076
  6.4 11.2 %copy-start.3 = (s32[256]{0:T(256)S(1)}, s32[256]{0:T(256)}, u32[]{:S(2)}) copy-start(s32[256]{0:T(256)} %param.8) | copy-start | bytes 3076
  9.3 85.2 %all-to-all-start = ((f32[8,256,256]{2,1,0:T(8,128)}), f32[8,256,256]{2,1,0:T(8,128)S(1)}, u32[]{:S(2)}, u32[]{:S(2)}) async-start(f32[8,256,256]{2,1,0:T(8,128)} %bitcast.23), calls=%async_computation | async-start | bytes 4194304 | tf_op jit(solution)/shard_map/all_to_all | solution.py:54
  96.2 20.5 %copy-start.1 = (f32[7]{0:T(128)S(1)}, f32[7]{0:T(128)}, u32[]{:S(2)}) copy-start(f32[7]{0:T(128)} %param.10) | copy-start | bytes 88
  112.3 11.4 %collective-permute-start.1 = (f32[3,256,256]{2,1,0:T(8,128)S(1)}, f32[3,256,256]{2,1,0:T(8,128)S(1)}, u32[]{:S(2)}, u32[]{:S(2)}) collective-permute-start(f32[3,256,256]{2,1,0:T(8,128)S(1)} %bitcast.28), channel_id=1, source_target_pairs={{1,0},{2,1},{3,2},{5,4},{6,5},{7,6},{9,8},{10,9},{11,10},{13,12},{... | collective-permute-start | bytes 2359304 | tf_op jit(solution)/shard_map/ppermute | solution.py:39
  114.2 13.3 %collective-permute-start = (f32[3,256,256]{2,1,0:T(8,128)S(1)}, f32[3,256,256]{2,1,0:T(8,128)S(1)}, u32[]{:S(2)}, u32[]{:S(2)}) collective-permute-start(f32[3,256,256]{2,1,0:T(8,128)S(1)} %bitcast.27), channel_id=1, source_target_pairs={{0,1},{1,2},{2,3},{4,5},{5,6},{6,7},{8,9},{9,10},{10,11},{12,13},{... | collective-permute-start | bytes 2359304 | tf_op jit(solution)/shard_map/ppermute | solution.py:38

commit v2 on v1

v2 whole, which is shorter than its diff:
```python
import functools

import jax
import jax.numpy as jnp
from jax import lax
from jax.sharding import PartitionSpec as P
from jax.experimental import pallas as pl
from jax.experimental.pallas import tpu as pltpu

OFFC = 80


def tap_table(filter_time, width_in, width_out):
    inner = jnp.arange(width_in, dtype=jnp.int32)[:, None]
    outer = jnp.arange(width_out, dtype=jnp.int32)[None, :]
    distance = inner - outer
    taps = jnp.arange(filter_time.shape[0], dtype=jnp.int32)
    matches = distance[:, :, None] == taps[None, None, :]
    return jnp.sum(jnp.where(matches, filter_time[None, None, :], 0.0), axis=2)


def block_filter(data, filter_time):
    reach = filter_time.shape[0] // 2
    block_width = 128
    leading = data.shape[:-1]
    samples = data.shape[-1]
    blocks = data.reshape(leading + (samples // block_width, block_width))
    zeroes = jnp.zeros(leading + (1, reach), jnp.float32)
    before = jnp.concatenate([zeroes, blocks[..., :-1, block_width - reach :]], axis=-2)
    after = jnp.concatenate([blocks[..., 1:, :reach], zeroes], axis=-2)
    extended = jnp.concatenate([before, blocks, after], axis=-1)
    table = tap_table(filter_time, block_width + 2 * reach, block_width)
    result = jnp.einsum("...ki,io->...ko", extended, table, precision=lax.Precision.HIGHEST)
    return result.reshape(leading + (samples,))


def mix_kernel(taps, filter_ref, ext_ref, out_ref):
    c = pl.program_id(0)
    acc = filter_ref[0] * ext_ref[c]
    for k in range(1, taps):
        acc = acc + filter_ref[k] * ext_ref[c + k]
    out_ref[0] = acc.T


def offset_mix(ext, filter_off, count):
    taps = filter_off.shape[0]
    _, rows, cols = ext.shape
    if rows % 128 or cols % 128:
        mixed = filter_off[0] * ext[0:count]
        for k in range(1, taps):
            mixed = mixed + filter_off[k] * ext[k : k + count]
        return jnp.transpose(mixed, (0, 2, 1))
    return pl.pallas_call(
        functools.partial(mix_kernel, taps),
        grid=(count,),
        in_specs=[
            pl.BlockSpec(memory_space=pltpu.SMEM),
            pl.BlockSpec(memory_space=pltpu.VMEM),
        ],
        out_specs=pl.BlockSpec((1, cols, rows), lambda c: (c, 0, 0)),
        out_shape=jax.ShapeDtypeStruct((count, cols, rows), jnp.float32),
    )(filter_off, ext)


def body(traces, cmp_bin, offset_class, bin_rank, filter_off, filter_time):
    shots = lax.axis_size("shot")
    off_count = lax.axis_size("off")
    off_dev = OFFC // off_count
    first_class = lax.axis_index("off") * off_dev
    bin_count = bin_rank.shape[0]
    tr_dev, samples = traces.shape
    window = samples // shots
    reach = filter_off.shape[0] // 2
    ext_classes = off_dev + 2 * reach

    place = jnp.take(bin_rank, cmp_bin, axis=0)
    cell = (offset_class - first_class + reach) * bin_count + place
    label_rows = -(-tr_dev // window)
    labels = jnp.pad(cell.astype(jnp.float32), (0, label_rows * window - tr_dev))
    labels = jnp.broadcast_to(labels.reshape(1, label_rows, window), (shots, label_rows, window))

    filtered = block_filter(traces, filter_time)
    outgoing = jnp.transpose(filtered.reshape(tr_dev, shots, window), (1, 0, 2))
    outgoing = jnp.concatenate([outgoing, labels], axis=1)
    received = lax.all_to_all(outgoing, "shot", 0, 0, tiled=True)
    rows = received[:, :tr_dev].reshape(shots * tr_dev, window)
    cells = received[:, tr_dev:].reshape(shots, label_rows * window)[:, :tr_dev]
    cells = cells.reshape(shots * tr_dev).astype(jnp.int32)

    fold = jnp.sum((cells[:, None] == cells[None, :]).astype(jnp.float32), axis=1)
    scale = 1.0 / jnp.maximum(fold, 1.0)
    stacked = jax.ops.segment_sum(rows * scale[:, None], cells, num_segments=ext_classes * bin_count)
    stacked = stacked.reshape(ext_classes, bin_count, window)

    ends = off_count - 1
    head = stacked[reach : 2 * reach]
    tail = stacked[off_dev : off_dev + reach]
    before = lax.ppermute(tail, "off", [(i, i + 1) for i in range(ends)])
    after = lax.ppermute(head, "off", [(i + 1, i) for i in range(ends)])
    ext = lax.dynamic_update_slice_in_dim(stacked, before, 0, axis=0)
    ext = lax.dynamic_update_slice_in_dim(ext, after, off_dev + reach, axis=0)
    return offset_mix(ext, filter_off, off_dev)


def solution(mesh):
    return jax.shard_map(
        body,
        mesh=mesh,
        in_specs=(P(("shot", "off"), None), P(("shot", "off")), P(("shot", "off")), P(), P(), P()),
        out_specs=P("off", "shot", None),
        check_vma=False,
    )
```

time: 153 us -> 117 us (0.76)
  the two profiles are of different devices: /device:TPU:10 before, /device:TPU:1 now
where the time goes in v2:
time: 117 us
  blocking collectives  55.6 us (48%)
  other arithmetic  18.5 us (16%)
  Pallas kernels  12.1 us (10%)
  waiting for transfers between devices  10.5 us (9%)
  local copies, waits for them, and re-layouts  9.46 us (8%)
  starting transfers between devices  6.75 us (6%)
  matrix products  3.56 us (3%)
    all_to_all x1, blocking collectives, body(): received = lax.all_to_all(outgoing, 'shot', 0, 0, tiled=True)  55.6 us
    scatter-add x1, other arithmetic, body(): jax.ops.segment_sum(rows * scale[:, None], cells, num_segments=ext_classe...  14.7 us
    pallas_call x1, Pallas kernels, offset_mix(): pl.pallas_call(functools.partial(mix_kernel, taps), grid=(count,), in_spe...  12.1 us
    ppermute x1, waiting for transfers between devices, body(): before = lax.ppermute(tail, 'off', [(i, i + 1) for i in range(ends)])  6.98 us
    ppermute x1, starting transfers between devices, body(): before = lax.ppermute(tail, 'off', [(i, i + 1) for i in range(ends)])  4.83 us
    dot_general x1, matrix products, block_filter(): jnp.einsum('...ki,io->...ko', extended, table, precision=lax.Precision.HI...  3.56 us
    ppermute x1, waiting for transfers between devices, body(): after = lax.ppermute(head, 'off', [(i + 1, i) for i in range(ends)])  3.47 us
  transfers between devices with their start and end apart: 2, of which 2 were waited for; matrix products, arithmetic and copies ran while one was open for 1% of the time, Pallas kernels for 0%

profile of v2, /device:TPU:1, one launch (start us, length us, event | category | flops | bytes accessed | tf_op | source)
XLA Modules:
  0.0 116.5 jit_solution(4597523495095465708)
XLA Ops:
  0.0 0.0 copy-start
  0.0 0.0 copy-start.3
  0.0 0.7 compare_select_fusion
  0.7 1.9 %copy.13 = f32[256,2048]{0,1:T(8,128)S(1)} copy(f32[256,2048]{1,0:T(8,128)} %param.6) | data formatting | bytes 4194304 | tf_op args[0]
  2.6 0.1 fusion.17
  2.8 0.0 copy-done.3
  2.8 0.8 select_reduce_fusion
  3.5 3.6 %fusion.2 = f32[256,16,128]{0,2,1:T(8,128)} fusion(f32[256,15,32]{0,2,1:T(8,128)S(1)} %get-tuple-element.8, f32[256,15,32]{0,2,1:T(8,128)S(1)} %get-tuple-element.7, f32[256,16,128]{0,2,1:T(8,128)S(1)} %bitcast.15, f32[192,128]{1,0:T(8,128)S(1)} %select_reduce_fusion), kind=kOutput, calls=%fused_computation.8 | convolution fusion | flops 1212678144 | bytes 5275648 | tf_op jit(solution)/shard_map/...ki,io->...ko/dot_general | solution.py:33
  7.1 0.0 copy-start.1
  7.1 0.0 copy-start.2
  7.1 1.9 %copy.14 = f32[256,8,256]{2,0,1:T(8,128)S(1)} copy(f32[256,8,256]{0,2,1:T(8,128)} %bitcast.16) | data formatting | bytes 4194304 | tf_op jit(solution)/shard_map/reshape;reshape | solution.py:83
  9.0 0.0 copy-done
  9.1 1.9 %gather_fusion = s32[256]{0:T(256)S(1)} fusion(s32[256]{0:T(256)S(1)} %copy-done, s32[1024]{0:T(1024)S(1)} %pad_clamp_fusion), kind=kCustom, calls=%fused_computation | custom fusion | bytes 3072 | tf_op jit(solution)/shard_map/jit(_take)/gather | solution.py:76
  11.0 0.0 copy-done.1
  11.0 0.0 copy-done.2
  11.1 0.1 pad_maximum_fusion
  11.2 55.6 %all_to_all.5 = f32[8,257,256]{2,1,0:T(8,128)S(1)} all-to-all(f32[8,257,256]{2,1,0:T(8,128)S(1)} %pad_maximum_fusion), channel_id=1, replica_groups=mesh['shot'=8,'off'=4] {'shot'}, dimensions={0} | all-to-all | bytes 4210688 | tf_op jit(solution)/shard_map/all_to_all | solution.py:85
  66.8 1.8 %convert_reduce_fusion = f32[2048]{0:T(1024)S(1)} fusion(s32[2048]{0:T(1024)S(1)} %bitcast.19), kind=kLoop, calls=%fused_computation.2 | loop fusion | flops 12580864 | bytes 16384 | tf_op jit(solution)/shard_map/reduce_sum | solution.py:90
  68.6 0.2 slice.37
  68.8 0.3 bitcast_multiply_fusion
  69.1 14.7 %scatter_custom_fusion = f32[6656,256]{1,0:T(8,128)} fusion(s32[2048]{0:T(1024)S(1)} %bitcast.20, f32[2048,256]{1,0:T(8,128)S(1)} %bitcast_multiply_fusion, f32[]{:T(128)} %constant.10.clone.1), kind=kCustom, calls=%fused_computation.5 | custom fusion | flops 524288 | bytes 6815748 | tf_op jit(solution)/shard_map/scatter-add | solution.py:92
  83.9 1.5 %fusion.16 = (f32[768,256]{1,0:T(8,128)S(1)}, f32[768,256]{1,0:T(8,128)S(1)}) fusion(f32[6656,256]{1,0:T(8,128)} %scatter_custom_fusion), kind=kLoop, calls=%fused_computation.35 | loop fusion | bytes 3145728 | tf_op jit(solution)/shard_map/slice | solution.py:96
  85.3 4.8 %collective-permute-start = (f32[3,256,256]{2,1,0:T(8,128)S(1)}, f32[3,256,256]{2,1,0:T(8,128)S(1)}, u32[]{:S(2)}, u32[]{:S(2)}) collective-permute-start(f32[3,256,256]{2,1,0:T(8,128)S(1)} %bitcast.18), channel_id=1, source_target_pairs={{0,1},{1,2},{2,3},{4,5},{5,6},{6,7},{8,9},{9,10},{10,11},{12,13},{... | collective-permute-start | bytes 2359304 | tf_op jit(solution)/shard_map/ppermute | solution.py:98
  90.2 1.9 %collective-permute-start.1 = (f32[3,256,256]{2,1,0:T(8,128)S(1)}, f32[3,256,256]{2,1,0:T(8,128)S(1)}, u32[]{:S(2)}, u32[]{:S(2)}) collective-permute-start(f32[3,256,256]{2,1,0:T(8,128)S(1)} %bitcast.17), channel_id=1, source_target_pairs={{1,0},{2,1},{3,2},{5,4},{6,5},{7,6},{9,8},{10,9},{11,10},{13,12},{... | collective-permute-start | bytes 2359304 | tf_op jit(solution)/shard_map/ppermute | solution.py:99
  92.1 7.0 %collective-permute-done = f32[3,256,256]{2,1,0:T(8,128)S(1)} collective-permute-done((f32[3,256,256]{2,1,0:T(8,128)S(1)}, f32[3,256,256]{2,1,0:T(8,128)S(1)}, u32[]{:S(2)}, u32[]{:S(2)}) %collective-permute-start) | collective-permute-done | bytes 786464 | tf_op jit(solution)/shard_map/ppermute | solution.py:98
  99.1 0.9 constant_dynamic-update-slice_fusion.1
  100.0 3.5 %collective-permute-done.1 = f32[3,256,256]{2,1,0:T(8,128)S(1)} collective-permute-done((f32[3,256,256]{2,1,0:T(8,128)S(1)}, f32[3,256,256]{2,1,0:T(8,128)S(1)}, u32[]{:S(2)}, u32[]{:S(2)}) %collective-permute-start.1) | collective-permute-done | bytes 786464 | tf_op jit(solution)/shard_map/ppermute | solution.py:99
  103.5 0.9 constant_dynamic-update-slice_fusion.ext_ref
  104.4 12.1 %shard_map.64 = f32[20,256,256]{2,1,0:T(8,128)} custom-call(f32[7]{0:T(128)} %filter_ref.1, f32[26,256,256]{2,1,0:T(8,128)} %constant_dynamic-update-slice_fusion.ext_ref), custom_call_target="tpu_custom_call" | custom-call | tf_op jit(solution)/shard_map/pallas_call | solution.py:53
  (6 shorter events, 0.1 us)
Async XLA Ops:
  0.0 9.0 %copy-start = (s32[256]{0:T(256)S(1)}, s32[256]{0:T(256)}, u32[]{:S(2)}) copy-start(s32[256]{0:T(256)} %param.9) | copy-start | bytes 3076
  0.0 2.8 %copy-start.3 = (f32[65]{0:T(128)S(1)}, f32[65]{0:T(128)}, u32[]{:S(2)}) copy-start(f32[65]{0:T(128)} %param.11) | copy-start | bytes 784
  7.1 3.9 %copy-start.1 = (s32[256]{0:T(256)S(1)}, s32[256]{0:T(256)}, u32[]{:S(2)}) copy-start(s32[256]{0:T(256)} %param.7) | copy-start | bytes 3076
  7.1 3.9 %copy-start.2 = (s32[256]{0:T(256)S(1)}, s32[256]{0:T(256)}, u32[]{:S(2)}) copy-start(s32[256]{0:T(256)} %param.8) | copy-start | bytes 3076
  85.3 13.8 %collective-permute-start = (f32[3,256,256]{2,1,0:T(8,128)S(1)}, f32[3,256,256]{2,1,0:T(8,128)S(1)}, u32[]{:S(2)}, u32[]{:S(2)}) collective-permute-start(f32[3,256,256]{2,1,0:T(8,128)S(1)} %bitcast.18), channel_id=1, source_target_pairs={{0,1},{1,2},{2,3},{4,5},{5,6},{6,7},{8,9},{9,10},{10,11},{12,13},{... | collective-permute-start | bytes 2359304 | tf_op jit(solution)/shard_map/ppermute | solution.py:98
  90.2 13.3 %collective-permute-start.1 = (f32[3,256,256]{2,1,0:T(8,128)S(1)}, f32[3,256,256]{2,1,0:T(8,128)S(1)}, u32[]{:S(2)}, u32[]{:S(2)}) collective-permute-start(f32[3,256,256]{2,1,0:T(8,128)S(1)} %bitcast.17), channel_id=1, source_target_pairs={{1,0},{2,1},{3,2},{5,4},{6,5},{7,6},{9,8},{10,9},{11,10},{13,12},{... | collective-permute-start | bytes 2359304 | tf_op jit(solution)/shard_map/ppermute | solution.py:99

commit v3 on v2

--- a/solution.py
+++ b/solution.py
@@ -34,30 +34,31 @@
     return result.reshape(leading + (samples,))
 
 
-def mix_kernel(taps, filter_ref, ext_ref, out_ref):
-    c = pl.program_id(0)
-    acc = filter_ref[0] * ext_ref[c]
-    for k in range(1, taps):
-        acc = acc + filter_ref[k] * ext_ref[c + k]
-    out_ref[0] = acc.T
+def mix_kernel(taps, count, filter_ref, ext_ref, out_ref):
+    for c in range(count):
+        acc = filter_ref[0] * ext_ref[c]
+        for k in range(1, taps):
+            acc = acc + filter_ref[k] * ext_ref[c + k]
+        out_ref[c] = acc.T
 
 
 def offset_mix(ext, filter_off, count):
     taps = filter_off.shape[0]
-    _, rows, cols = ext.shape
+    classes, rows, cols = ext.shape
     if rows % 128 or cols % 128:
         mixed = filter_off[0] * ext[0:count]
         for k in range(1, taps):
             mixed = mixed + filter_off[k] * ext[k : k + count]
         return jnp.transpose(mixed, (0, 2, 1))
+    tile = 128
     return pl.pallas_call(
-        functools.partial(mix_kernel, taps),
-        grid=(count,),
+        functools.partial(mix_kernel, taps, count),
+        grid=(rows // tile, cols // tile),
         in_specs=[
             pl.BlockSpec(memory_space=pltpu.SMEM),
-            pl.BlockSpec(memory_space=pltpu.VMEM),
+            pl.BlockSpec((classes, tile, tile), lambda i, j: (0, i, j)),
         ],
-        out_specs=pl.BlockSpec((1, cols, rows), lambda c: (c, 0, 0)),
+        out_specs=pl.BlockSpec((count, tile, tile), lambda i, j: (0, j, i)),
         out_shape=jax.ShapeDtypeStruct((count, cols, rows), jnp.float32),
     )(filter_off, ext)
 
@@ -72,6 +73,8 @@
     window = samples // shots
     reach = filter_off.shape[0] // 2
     ext_classes = off_dev + 2 * reach
+    halves = 2 if tr_dev % 16 == 0 else 1
+    part = tr_dev // halves
 
     place = jnp.take(bin_rank, cmp_bin, axis=0)
     cell = (offset_class - first_class + reach) * bin_count + place
@@ -79,17 +82,24 @@
     labels = jnp.pad(cell.astype(jnp.float32), (0, label_rows * window - tr_dev))
     labels = jnp.broadcast_to(labels.reshape(1, label_rows, window), (shots, label_rows, window))
 
-    filtered = block_filter(traces, filter_time)
-    outgoing = jnp.transpose(filtered.reshape(tr_dev, shots, window), (1, 0, 2))
-    outgoing = jnp.concatenate([outgoing, labels], axis=1)
-    received = lax.all_to_all(outgoing, "shot", 0, 0, tiled=True)
-    rows = received[:, :tr_dev].reshape(shots * tr_dev, window)
-    cells = received[:, tr_dev:].reshape(shots, label_rows * window)[:, :tr_dev]
-    cells = cells.reshape(shots * tr_dev).astype(jnp.int32)
+    pieces = []
+    for h in range(halves):
+        filtered = block_filter(traces[h * part : (h + 1) * part], filter_time)
+        outgoing = jnp.transpose(filtered.reshape(part, shots, window), (1, 0, 2))
+        if h == 0:
+            outgoing = jnp.concatenate([outgoing, labels], axis=1)
+        pieces.append(lax.all_to_all(outgoing, "shot", 0, 0, tiled=True))
+    cells = pieces[0][:, part:].reshape(shots, label_rows * window)[:, :tr_dev]
+    cells = cells.astype(jnp.int32)
+    flat = cells.reshape(shots * tr_dev)
+    fold = jnp.sum((flat[:, None] == flat[None, :]).astype(jnp.float32), axis=1)
+    scale = (1.0 / jnp.maximum(fold, 1.0)).reshape(shots, tr_dev)
 
-    fold = jnp.sum((cells[:, None] == cells[None, :]).astype(jnp.float32), axis=1)
-    scale = 1.0 / jnp.maximum(fold, 1.0)
-    stacked = jax.ops.segment_sum(rows * scale[:, None], cells, num_segments=ext_classes * bin_count)
+    stacked = jnp.zeros((ext_classes * bin_count, window), jnp.float32)
+    for h in range(halves):
+        rows = pieces[h][:, :part] * scale[:, h * part : (h + 1) * part, None]
+        index = cells[:, h * part : (h + 1) * part].reshape(shots * part)
+        stacked = stacked.at[index].add(rows.reshape(shots * part, window))
     stacked = stacked.reshape(ext_classes, bin_count, window)
 
     ends = off_count - 1

time: 117 us -> 120 us (1.026)
  blocking collectives: 55.6 us -> 0 us
  waiting for transfers between devices: 10.5 us -> 57.5 us
  starting transfers between devices: 6.75 us -> 17.6 us
  other arithmetic: 18.5 us -> 25.6 us
  Pallas kernels: 12.1 us -> 6.94 us
    all_to_all x1 -> x0, blocking collectives: 55.6 us -> none  [body(): received = lax.all_to_all(outgoing, 'shot', 0, 0, tiled=True)]
    all_to_all x0 -> x2, waiting for transfers between devices: none -> 47 us  [body(): pieces.append(lax.all_to_all(outgoing, 'shot', 0, 0, tiled=True))]
    all_to_all x0 -> x2, starting transfers between devices: none -> 11.1 us  [body(): pieces.append(lax.all_to_all(outgoing, 'shot', 0, 0, tiled=True))]
    scatter-add x1 -> x2, other arithmetic: 14.7 us -> 20.9 us  [body(): stacked = stacked.at[index].add(rows.reshape(shots * part, window))]
    pallas_call x1, Pallas kernels: 12.1 us -> 6.94 us  [offset_mix(): pl.pallas_call(functools.partial(mix_kernel, taps, count), grid=(rows //...]
    slice x1 -> x6, local copies, waits for them, and re-layouts: 0.18 us -> 2.34 us  [the longest x3 2.32 us: body(): filtered = block_filter(traces[h * part:(h + 1) * part], filter_time)]
    unnamed x9, local copies, waits for them, and re-layouts: 1.93 us -> 0.3 us
    another operation x1, local copies, waits for them, and re-layouts: 1.95 us -> 0.33 us  [body(): outgoing = jnp.transpose(filtered.reshape(part, shots, window), (1, 0, 2))]
  transfers between devices with their start and end apart: 2 -> 4, of which waited for: 2 -> 4; matrix products, arithmetic and copies ran while one was open for 1% -> 4% of each run, Pallas kernels for 0% -> 0%
where the time goes in v3:
time: 120 us
  waiting for transfers between devices  57.5 us (48%)
  other arithmetic  25.6 us (21%)
  starting transfers between devices  17.6 us (15%)
  local copies, waits for them, and re-layouts  8.69 us (7%)
  Pallas kernels  6.94 us (6%)
  matrix products  3.37 us (3%)
    all_to_all x2, waiting for transfers between devices, body(): pieces.append(lax.all_to_all(outgoing, 'shot', 0, 0, tiled=True))  47 us
    scatter-add x2, other arithmetic, body(): stacked = stacked.at[index].add(rows.reshape(shots * part, window))  20.9 us
    all_to_all x2, starting transfers between devices, body(): pieces.append(lax.all_to_all(outgoing, 'shot', 0, 0, tiled=True))  11.1 us
    ppermute x1, waiting for transfers between devices, body(): before = lax.ppermute(tail, 'off', [(i, i + 1) for i in range(ends)])  6.98 us
    pallas_call x1, Pallas kernels, offset_mix(): pl.pallas_call(functools.partial(mix_kernel, taps, count), grid=(rows //...  6.94 us
    ppermute x1, starting transfers between devices, body(): before = lax.ppermute(tail, 'off', [(i, i + 1) for i in range(ends)])  4.62 us
    ppermute x1, waiting for transfers between devices, body(): after = lax.ppermute(head, 'off', [(i + 1, i) for i in range(ends)])  3.45 us
    dot_general x2, matrix products, block_filter(): jnp.einsum('...ki,io->...ko', extended, table, precision=lax.Precision.HI...  3.37 us
  transfers between devices with their start and end apart: 4, of which 4 were waited for; matrix products, arithmetic and copies ran while one was open for 4% of the time, Pallas kernels for 0%

profile of v3, /device:TPU:1, one launch (start us, length us, event | category | flops | bytes accessed | tf_op | source)
XLA Modules:
  0.0 119.9 jit_solution(1065293959532840597)
XLA Ops:
  0.0 0.0 copy-start
  0.0 0.7 compare_select_fusion.2
  0.7 1.7 %fusion.31 = (f32[128,2048]{1,0:T(8,128)S(1)}, f32[128,2048]{1,0:T(8,128)S(1)}) fusion(f32[256,2048]{1,0:T(8,128)} %param.6), kind=kLoop, calls=%fused_computation.56 | loop fusion | bytes 4194304 | tf_op jit(solution)/shard_map/slice | solution.py:87
  2.4 0.0 copy-start.3
  2.4 0.3 copy.27
  2.8 0.3 copy-done.3
  3.1 0.8 select_reduce_fusion
  3.8 1.2 fusion.5
  5.0 0.0 copy-start.1
  5.0 0.0 copy-start.2
  5.0 0.3 copy.28
  5.4 0.0 copy-done
  5.4 1.9 %gather_fusion = s32[256]{0:T(256)S(1)} fusion(s32[256]{0:T(256)S(1)} %copy-done, s32[1024]{0:T(1024)S(1)} %pad_clamp_fusion), kind=kCustom, calls=%fused_computation | custom fusion | bytes 3072 | tf_op jit(solution)/shard_map/jit(_take)/gather | solution.py:79
  7.4 0.0 copy-done.1
  7.4 0.0 copy-done.2
  7.4 1.1 pad_maximum_fusion
  8.5 6.4 %all-to-all-start = ((f32[8,129,256]{2,1,0:T(8,128)}), f32[8,129,256]{2,1,0:T(8,128)S(1)}, u32[]{:S(2)}, u32[]{:S(2)}) async-start(f32[8,129,256]{2,1,0:T(8,128)} %pad_maximum_fusion), calls=%async_computation | async-start | bytes 2228224 | tf_op jit(solution)/shard_map/all_to_all | solution.py:91
  14.9 0.3 copy.30
  15.3 2.2 %fusion.2 = f32[128,16,128]{0,2,1:T(8,128)} fusion(f32[128,15,32]{0,2,1:T(8,128)S(1)} %get-tuple-element.10, f32[128,15,32]{0,2,1:T(8,128)S(1)} %get-tuple-element.9, f32[128,16,128]{0,2,1:T(8,128)S(1)} %bitcast.33, f32[192,128]{1,0:T(8,128)S(1)} %select_reduce_fusion), kind=kOutput, calls=%fused_computation.9 | convolution fusion | flops 606339072 | bytes 2686976 | tf_op jit(solution)/shard_map/...ki,io->...ko/dot_general | solution.py:33
  17.4 23.8 %all-to-all-done = f32[8,129,256]{2,1,0:T(8,128)S(1)} async-done(((f32[8,129,256]{2,1,0:T(8,128)}), f32[8,129,256]{2,1,0:T(8,128)S(1)}, u32[]{:S(2)}, u32[]{:S(2)}) %all-to-all-start) | async-done | bytes 1056800 | tf_op jit(solution)/shard_map/all_to_all | solution.py:91
  41.2 4.7 %all-to-all-start.1 = ((f32[8,128,256]{1,2,0:T(8,128)}), f32[8,128,256]{1,2,0:T(8,128)S(1)}, u32[]{:S(2)}, u32[]{:S(2)}) async-start(f32[8,128,256]{1,2,0:T(8,128)} %bitcast.34), calls=%async_computation.1 | async-start | bytes 2097152 | tf_op jit(solution)/shard_map/all_to_all | solution.py:91
  45.9 1.8 %convert_reduce_fusion = f32[2048]{0:T(1024)S(1)} fusion(s32[2048]{0:T(1024)S(1)} %bitcast.42), kind=kLoop, calls=%fused_computation.3 | loop fusion | flops 12580864 | bytes 16384 | tf_op jit(solution)/shard_map/reduce_sum | solution.py:95
  47.7 23.3 %all-to-all-done.1 = f32[8,128,256]{1,2,0:T(8,128)S(1)} async-done(((f32[8,128,256]{1,2,0:T(8,128)}), f32[8,128,256]{1,2,0:T(8,128)S(1)}, u32[]{:S(2)}, u32[]{:S(2)}) %all-to-all-start.1) | async-done | bytes 1048608 | tf_op jit(solution)/shard_map/all_to_all | solution.py:91
  71.0 0.1 broadcast_multiply_fusion
  71.1 0.3 copy.31
  71.5 0.2 slice_multiply_fusion
  71.7 9.2 %scatter_custom_fusion = f32[6656,256]{1,0:T(8,128)} fusion(s32[1024]{0:T(1024)S(1)} %bitcast.43, f32[1024,256]{1,0:T(8,128)S(1)} %bitcast.35, f32[]{:T(128)} %constant.11.clone.1), kind=kCustom, calls=%fused_computation.6 | custom fusion | flops 262144 | bytes 6815748 | tf_op jit(solution)/shard_map/scatter-add | solution.py:102
  80.9 11.7 %scatter_fusion = f32[6656,256]{1,0:T(8,128)} fusion(f32[6656,256]{1,0:T(8,128)} %scatter_custom_fusion, s32[1024]{0:T(1024)S(1)} %bitcast.39, f32[1024,256]{1,0:T(8,128)S(1)} %bitcast.28), kind=kCustom, calls=%fused_computation.2 | custom fusion | flops 262144 | bytes 3149824 | tf_op jit(solution)/shard_map/scatter-add | solution.py:102
  92.6 1.5 %fusion.30 = (f32[768,256]{1,0:T(8,128)S(1)}, f32[768,256]{1,0:T(8,128)S(1)}) fusion(f32[6656,256]{1,0:T(8,128)} %scatter_fusion), kind=kLoop, calls=%fused_computation.55 | loop fusion | bytes 3145728 | tf_op jit(solution)/shard_map/slice | solution.py:106
  94.1 4.6 %collective-permute-start = (f32[3,256,256]{2,1,0:T(8,128)S(1)}, f32[3,256,256]{2,1,0:T(8,128)S(1)}, u32[]{:S(2)}, u32[]{:S(2)}) collective-permute-start(f32[3,256,256]{2,1,0:T(8,128)S(1)} %bitcast.38), channel_id=1, source_target_pairs={{0,1},{1,2},{2,3},{4,5},{5,6},{6,7},{8,9},{9,10},{10,11},{12,13},{... | collective-permute-start | bytes 2359304 | tf_op jit(solution)/shard_map/ppermute | solution.py:108
  98.7 1.9 %collective-permute-start.1 = (f32[3,256,256]{2,1,0:T(8,128)S(1)}, f32[3,256,256]{2,1,0:T(8,128)S(1)}, u32[]{:S(2)}, u32[]{:S(2)}) collective-permute-start(f32[3,256,256]{2,1,0:T(8,128)S(1)} %bitcast.37), channel_id=1, source_target_pairs={{1,0},{2,1},{3,2},{5,4},{6,5},{7,6},{9,8},{10,9},{11,10},{13,12},{... | collective-permute-start | bytes 2359304 | tf_op jit(solution)/shard_map/ppermute | solution.py:109
  100.6 7.0 %collective-permute-done = f32[3,256,256]{2,1,0:T(8,128)S(1)} collective-permute-done((f32[3,256,256]{2,1,0:T(8,128)S(1)}, f32[3,256,256]{2,1,0:T(8,128)S(1)}, u32[]{:S(2)}, u32[]{:S(2)}) %collective-permute-start) | collective-permute-done | bytes 786464 | tf_op jit(solution)/shard_map/ppermute | solution.py:108
  107.6 0.9 constant_dynamic-update-slice_fusion.1
  108.6 3.4 %collective-permute-done.1 = f32[3,256,256]{2,1,0:T(8,128)S(1)} collective-permute-done((f32[3,256,256]{2,1,0:T(8,128)S(1)}, f32[3,256,256]{2,1,0:T(8,128)S(1)}, u32[]{:S(2)}, u32[]{:S(2)}) %collective-permute-start.1) | collective-permute-done | bytes 786464 | tf_op jit(solution)/shard_map/ppermute | solution.py:109
  112.0 0.9 constant_dynamic-update-slice_fusion.ext_ref
  113.0 6.9 %shard_map.64 = f32[20,256,256]{2,1,0:T(8,128)} custom-call(f32[7]{0:T(128)} %filter_ref.1, f32[26,256,256]{2,1,0:T(8,128)} %constant_dynamic-update-slice_fusion.ext_ref), custom_call_target="tpu_custom_call" | custom-call | tf_op jit(solution)/shard_map/pallas_call | solution.py:54
  (15 shorter events, 0.2 us)
Async XLA Ops:
  0.0 5.4 %copy-start = (s32[256]{0:T(256)S(1)}, s32[256]{0:T(256)}, u32[]{:S(2)}) copy-start(s32[256]{0:T(256)} %param.9) | copy-start | bytes 3076
  2.4 0.7 copy-start.3
  5.0 2.3 %copy-start.1 = (s32[256]{0:T(256)S(1)}, s32[256]{0:T(256)}, u32[]{:S(2)}) copy-start(s32[256]{0:T(256)} %param.7) | copy-start | bytes 3076
  5.0 2.3 %copy-start.2 = (s32[256]{0:T(256)S(1)}, s32[256]{0:T(256)}, u32[]{:S(2)}) copy-start(s32[256]{0:T(256)} %param.8) | copy-start | bytes 3076
  8.5 32.7 %all-to-all-start = ((f32[8,129,256]{2,1,0:T(8,128)}), f32[8,129,256]{2,1,0:T(8,128)S(1)}, u32[]{:S(2)}, u32[]{:S(2)}) async-start(f32[8,129,256]{2,1,0:T(8,128)} %pad_maximum_fusion), calls=%async_computation | async-start | bytes 2228224 | tf_op jit(solution)/shard_map/all_to_all | solution.py:91
  41.2 29.8 %all-to-all-start.1 = ((f32[8,128,256]{1,2,0:T(8,128)}), f32[8,128,256]{1,2,0:T(8,128)S(1)}, u32[]{:S(2)}, u32[]{:S(2)}) async-start(f32[8,128,256]{1,2,0:T(8,128)} %bitcast.34), calls=%async_computation.1 | async-start | bytes 2097152 | tf_op jit(solution)/shard_map/all_to_all | solution.py:91
  94.1 13.5 %collective-permute-start = (f32[3,256,256]{2,1,0:T(8,128)S(1)}, f32[3,256,256]{2,1,0:T(8,128)S(1)}, u32[]{:S(2)}, u32[]{:S(2)}) collective-permute-start(f32[3,256,256]{2,1,0:T(8,128)S(1)} %bitcast.38), channel_id=1, source_target_pairs={{0,1},{1,2},{2,3},{4,5},{5,6},{6,7},{8,9},{9,10},{10,11},{12,13},{... | collective-permute-start | bytes 2359304 | tf_op jit(solution)/shard_map/ppermute | solution.py:108
  98.7 13.3 %collective-permute-start.1 = (f32[3,256,256]{2,1,0:T(8,128)S(1)}, f32[3,256,256]{2,1,0:T(8,128)S(1)}, u32[]{:S(2)}, u32[]{:S(2)}) collective-permute-start(f32[3,256,256]{2,1,0:T(8,128)S(1)} %bitcast.37), channel_id=1, source_target_pairs={{1,0},{2,1},{3,2},{5,4},{6,5},{7,6},{9,8},{10,9},{11,10},{13,12},{... | collective-permute-start | bytes 2359304 | tf_op jit(solution)/shard_map/ppermute | solution.py:109

commit v4 on v2

--- a/solution.py
+++ b/solution.py
@@ -34,32 +34,60 @@
     return result.reshape(leading + (samples,))
 
 
-def mix_kernel(taps, filter_ref, ext_ref, out_ref):
-    c = pl.program_id(0)
-    acc = filter_ref[0] * ext_ref[c]
-    for k in range(1, taps):
-        acc = acc + filter_ref[k] * ext_ref[c + k]
-    out_ref[0] = acc.T
+def mix_kernel(taps, count, filter_ref, ext_ref, out_ref):
+    for c in range(count):
+        acc = filter_ref[0] * ext_ref[c]
+        for k in range(1, taps):
+            acc = acc + filter_ref[k] * ext_ref[c + k]
+        out_ref[c] = acc.T
 
 
 def offset_mix(ext, filter_off, count):
     taps = filter_off.shape[0]
-    _, rows, cols = ext.shape
+    classes, rows, cols = ext.shape
     if rows % 128 or cols % 128:
         mixed = filter_off[0] * ext[0:count]
         for k in range(1, taps):
             mixed = mixed + filter_off[k] * ext[k : k + count]
         return jnp.transpose(mixed, (0, 2, 1))
+    tile = 128
     return pl.pallas_call(
-        functools.partial(mix_kernel, taps),
-        grid=(count,),
+        functools.partial(mix_kernel, taps, count),
+        grid=(rows // tile, cols // tile),
         in_specs=[
+            pl.BlockSpec(memory_space=pltpu.SMEM),
+            pl.BlockSpec((classes, tile, tile), lambda i, j: (0, i, j)),
+        ],
+        out_specs=pl.BlockSpec((count, tile, tile), lambda i, j: (0, j, i)),
+        out_shape=jax.ShapeDtypeStruct((count, cols, rows), jnp.float32),
+    )(filter_off, ext)
+
+
+def scatter_kernel(count, cell_ref, scale_ref, rows_ref, out_ref):
+    out_ref[...] = jnp.zeros(out_ref.shape, jnp.float32)
+
+    def step(r, carry):
+        x = cell_ref[r]
+        out_ref[pl.ds(x, 1), :] += rows_ref[pl.ds(r, 1), :] * scale_ref[r]
+        return carry
+
+    lax.fori_loop(0, count, step, 0, unroll=8)
+
+
+def stack_rows(rows, cells, scale, segments):
+    count, width = rows.shape
+    if width % 128:
+        return jax.ops.segment_sum(rows * scale[:, None], cells, num_segments=segments)
+    return pl.pallas_call(
+        functools.partial(scatter_kernel, count),
+        in_specs=[
+            pl.BlockSpec(memory_space=pltpu.SMEM),
             pl.BlockSpec(memory_space=pltpu.SMEM),
             pl.BlockSpec(memory_space=pltpu.VMEM),
         ],
-        out_specs=pl.BlockSpec((1, cols, rows), lambda c: (c, 0, 0)),
-        out_shape=jax.ShapeDtypeStruct((count, cols, rows), jnp.float32),
-    )(filter_off, ext)
+        out_specs=pl.BlockSpec(memory_space=pltpu.VMEM),
+        out_shape=jax.ShapeDtypeStruct((segments, width), jnp.float32),
+    )(cells, scale, rows)
 
 
 def body(traces, cmp_bin, offset_class, bin_rank, filter_off, filter_time):
@@ -73,7 +101,8 @@
     reach = filter_off.shape[0] // 2
     ext_classes = off_dev + 2 * reach
 
-    place = jnp.take(bin_rank, cmp_bin, axis=0)
+    matches = cmp_bin[:, None] == jnp.arange(bin_count, dtype=jnp.int32)[None, :]
+    place = jnp.sum(jnp.where(matches, bin_rank[None, :], 0), axis=1)
     cell = (offset_class - first_class + reach) * bin_count + place
     label_rows = -(-tr_dev // window)
     labels = jnp.pad(cell.astype(jnp.float32), (0, label_rows * window - tr_dev))
@@ -89,7 +118,7 @@
 
     fold = jnp.sum((cells[:, None] == cells[None, :]).astype(jnp.float32), axis=1)
     scale = 1.0 / jnp.maximum(fold, 1.0)
-    stacked = jax.ops.segment_sum(rows * scale[:, None], cells, num_segments=ext_classes * bin_count)
+    stacked = stack_rows(rows, cells, scale, ext_classes * bin_count)
     stacked = stacked.reshape(ext_classes, bin_count, window)
 
     ends = off_count - 1

time: 117 us -> 110 us (0.940)
  other arithmetic: 18.5 us -> 3.49 us
  Pallas kernels: 12.1 us -> 21.2 us
    scatter-add x1 -> x0, other arithmetic: 14.7 us -> none  [body(): jax.ops.segment_sum(rows * scale[:, None], cells, num_segments=ext_classe...]
    pallas_call x1 -> x2, Pallas kernels: 12.1 us -> 21.2 us  [the longest x1 14.3 us: stack_rows(): pl.pallas_call(functools.partial(scatter_kernel, count), in_specs=[pl.Blo...]
    gather x1 -> x0, local copies, waits for them, and re-layouts: 1.95 us -> none  [body(): place = jnp.take(bin_rank, cmp_bin, axis=0)]
    slice x1, local copies, waits for them, and re-layouts: 0.18 us -> 1.53 us  [body(): rows = received[:, :tr_dev].reshape(shots * tr_dev, window)]
where the time goes in v4:
time: 110 us
  blocking collectives  55.6 us (51%)
  Pallas kernels  21.2 us (19%)
  waiting for transfers between devices  10.4 us (9%)
  local copies, waits for them, and re-layouts  8.88 us (8%)
  starting transfers between devices  6.75 us (6%)
  matrix products  3.55 us (3%)
  other arithmetic  3.49 us (3%)
    all_to_all x1, blocking collectives, body(): received = lax.all_to_all(outgoing, 'shot', 0, 0, tiled=True)  55.6 us
    pallas_call x1, Pallas kernels, stack_rows(): pl.pallas_call(functools.partial(scatter_kernel, count), in_specs=[pl.Blo...  14.3 us
    ppermute x1, waiting for transfers between devices, body(): before = lax.ppermute(tail, 'off', [(i, i + 1) for i in range(ends)])  6.98 us
    pallas_call x1, Pallas kernels, offset_mix(): pl.pallas_call(functools.partial(mix_kernel, taps, count), grid=(rows //...  6.94 us
    ppermute x1, starting transfers between devices, body(): before = lax.ppermute(tail, 'off', [(i, i + 1) for i in range(ends)])  4.83 us
    dot_general x1, matrix products, block_filter(): jnp.einsum('...ki,io->...ko', extended, table, precision=lax.Precision.HI...  3.55 us
    ppermute x1, waiting for transfers between devices, body(): after = lax.ppermute(head, 'off', [(i + 1, i) for i in range(ends)])  3.46 us
  transfers between devices with their start and end apart: 2, of which 2 were waited for; matrix products, arithmetic and copies ran while one was open for 1% of the time, Pallas kernels for 0%

profile of v4, /device:TPU:1, one launch (start us, length us, event | category | flops | bytes accessed | tf_op | source)
XLA Modules:
  0.0 110.0 jit_solution(16407203299177762608)
XLA Ops:
  0.0 0.0 copy-start.4
  0.0 1.9 %copy.9 = f32[256,2048]{0,1:T(8,128)S(1)} copy(f32[256,2048]{1,0:T(8,128)} %param.6) | data formatting | bytes 4194304 | tf_op args[0]
  1.9 0.1 fusion.13
  2.1 0.0 copy-done.4
  2.1 0.8 select_reduce_fusion
  2.8 3.6 %fusion = f32[256,16,128]{0,2,1:T(8,128)} fusion(f32[256,15,32]{0,2,1:T(8,128)S(1)} %get-tuple-element.8, f32[256,15,32]{0,2,1:T(8,128)S(1)} %get-tuple-element.7, f32[256,16,128]{0,2,1:T(8,128)S(1)} %bitcast.15, f32[192,128]{1,0:T(8,128)S(1)} %select_reduce_fusion), kind=kOutput, calls=%fused_computation.4 | convolution fusion | flops 1212678144 | bytes 5275648 | tf_op jit(solution)/shard_map/...ki,io->...ko/dot_general | solution.py:33
  6.4 0.0 copy-start.1
  6.4 0.0 copy-start.2
  6.4 0.0 copy-start.3
  6.4 2.0 %copy.10 = f32[256,8,256]{2,0,1:T(8,128)S(1)} copy(f32[256,8,256]{0,2,1:T(8,128)} %bitcast.16) | data formatting | bytes 4194304 | tf_op jit(solution)/shard_map/reshape;reshape | solution.py:112
  8.4 0.0 copy-done.1
  8.4 0.0 copy-done.2
  8.4 0.2 select_reduce_fusion.1
  8.6 0.0 copy-done.3
  8.6 0.1 pad_maximum_fusion
  8.7 55.6 %all_to_all.5 = f32[8,257,256]{2,1,0:T(8,128)S(1)} all-to-all(f32[8,257,256]{2,1,0:T(8,128)S(1)} %pad_maximum_fusion), channel_id=1, replica_groups=mesh['shot'=8,'off'=4] {'shot'}, dimensions={0} | all-to-all | bytes 4210688 | tf_op jit(solution)/shard_map/all_to_all | solution.py:114
  64.3 0.0 copy-start
  64.4 1.8 %convert_reduce_fusion = f32[2048]{0:T(1024)S(1)} fusion(s32[2048]{0:T(1024)S(1)} %bitcast.19), kind=kLoop, calls=%fused_computation | loop fusion | flops 12580864 | bytes 16384 | tf_op jit(solution)/shard_map/reduce_sum | solution.py:119
  66.1 0.6 maximum_divide_fusion.scale_ref
  66.7 1.5 %slice.35 = f32[8,256,256]{2,1,0:T(8,128)} slice(f32[8,257,256]{2,1,0:T(8,128)S(1)} %all_to_all.5), slice={[0:8], [0:256], [0:256]} | slice | bytes 4194304 | tf_op jit(solution)/shard_map/slice | solution.py:115
  68.3 0.0 copy-done
  68.3 14.3 %shard_map.64 = f32[6656,256]{1,0:T(8,128)} custom-call(s32[2048]{0:T(1024)} %bitcast.20, f32[2048]{0:T(1024)} %maximum_divide_fusion.scale_ref, f32[2048,256]{1,0:T(8,128)} %bitcast.12), custom_call_target="tpu_custom_call" | custom-call | tf_op jit(solution)/shard_map/pallas_call | solution.py:81
  82.5 1.5 %fusion.12 = (f32[768,256]{1,0:T(8,128)S(1)}, f32[768,256]{1,0:T(8,128)S(1)}) fusion(f32[6656,256]{1,0:T(8,128)} %shard_map.64), kind=kLoop, calls=%fused_computation.28 | loop fusion | bytes 3145728 | tf_op jit(solution)/shard_map/slice | solution.py:125
  84.0 4.8 %collective-permute-start = (f32[3,256,256]{2,1,0:T(8,128)S(1)}, f32[3,256,256]{2,1,0:T(8,128)S(1)}, u32[]{:S(2)}, u32[]{:S(2)}) collective-permute-start(f32[3,256,256]{2,1,0:T(8,128)S(1)} %bitcast.18), channel_id=1, source_target_pairs={{0,1},{1,2},{2,3},{4,5},{5,6},{6,7},{8,9},{9,10},{10,11},{12,13},{... | collective-permute-start | bytes 2359304 | tf_op jit(solution)/shard_map/ppermute | solution.py:127
  88.8 1.9 %collective-permute-start.1 = (f32[3,256,256]{2,1,0:T(8,128)S(1)}, f32[3,256,256]{2,1,0:T(8,128)S(1)}, u32[]{:S(2)}, u32[]{:S(2)}) collective-permute-start(f32[3,256,256]{2,1,0:T(8,128)S(1)} %bitcast.17), channel_id=1, source_target_pairs={{1,0},{2,1},{3,2},{5,4},{6,5},{7,6},{9,8},{10,9},{11,10},{13,12},{... | collective-permute-start | bytes 2359304 | tf_op jit(solution)/shard_map/ppermute | solution.py:128
  90.8 7.0 %collective-permute-done = f32[3,256,256]{2,1,0:T(8,128)S(1)} collective-permute-done((f32[3,256,256]{2,1,0:T(8,128)S(1)}, f32[3,256,256]{2,1,0:T(8,128)S(1)}, u32[]{:S(2)}, u32[]{:S(2)}) %collective-permute-start) | collective-permute-done | bytes 786464 | tf_op jit(solution)/shard_map/ppermute | solution.py:127
  97.7 0.9 constant_dynamic-update-slice_fusion.1
  98.7 3.5 %collective-permute-done.1 = f32[3,256,256]{2,1,0:T(8,128)S(1)} collective-permute-done((f32[3,256,256]{2,1,0:T(8,128)S(1)}, f32[3,256,256]{2,1,0:T(8,128)S(1)}, u32[]{:S(2)}, u32[]{:S(2)}) %collective-permute-start.1) | collective-permute-done | bytes 786464 | tf_op jit(solution)/shard_map/ppermute | solution.py:128
  102.1 0.9 constant_dynamic-update-slice_fusion.ext_ref
  103.1 6.9 %shard_map.65 = f32[20,256,256]{2,1,0:T(8,128)} custom-call(f32[7]{0:T(128)} %filter_ref.1, f32[26,256,256]{2,1,0:T(8,128)} %constant_dynamic-update-slice_fusion.ext_ref), custom_call_target="tpu_custom_call" | custom-call | tf_op jit(solution)/shard_map/pallas_call | solution.py:54
  (4 shorter events, 0.0 us)
Async XLA Ops:
  0.0 2.1 %copy-start.4 = (f32[65]{0:T(128)S(1)}, f32[65]{0:T(128)}, u32[]{:S(2)}) copy-start(f32[65]{0:T(128)} %param.11) | copy-start | bytes 784
  6.4 2.0 %copy-start.1 = (s32[256]{0:T(256)S(1)}, s32[256]{0:T(256)}, u32[]{:S(2)}) copy-start(s32[256]{0:T(256)} %param.9) | copy-start | bytes 3076
  6.4 2.0 %copy-start.2 = (s32[256]{0:T(256)S(1)}, s32[256]{0:T(256)}, u32[]{:S(2)}) copy-start(s32[256]{0:T(256)} %param.7) | copy-start | bytes 3076
  6.4 2.2 %copy-start.3 = (s32[256]{0:T(256)S(1)}, s32[256]{0:T(256)}, u32[]{:S(2)}) copy-start(s32[256]{0:T(256)} %param.8) | copy-start | bytes 3076
  64.3 3.9 %copy-start = (s32[8,1,256]{2,1,0:T(1,128)}, s32[8,1,256]{2,1,0:T(1,128)S(1)}, u32[]{:S(2)}) copy-start(s32[8,1,256]{2,1,0:T(1,128)S(1)} %slice_convert_fusion) | copy-start | bytes 24580
  84.0 13.8 %collective-permute-start = (f32[3,256,256]{2,1,0:T(8,128)S(1)}, f32[3,256,256]{2,1,0:T(8,128)S(1)}, u32[]{:S(2)}, u32[]{:S(2)}) collective-permute-start(f32[3,256,256]{2,1,0:T(8,128)S(1)} %bitcast.18), channel_id=1, source_target_pairs={{0,1},{1,2},{2,3},{4,5},{5,6},{6,7},{8,9},{9,10},{10,11},{12,13},{... | collective-permute-start | bytes 2359304 | tf_op jit(solution)/shard_map/ppermute | solution.py:127
  88.8 13.3 %collective-permute-start.1 = (f32[3,256,256]{2,1,0:T(8,128)S(1)}, f32[3,256,256]{2,1,0:T(8,128)S(1)}, u32[]{:S(2)}, u32[]{:S(2)}) collective-permute-start(f32[3,256,256]{2,1,0:T(8,128)S(1)} %bitcast.17), channel_id=1, source_target_pairs={{1,0},{2,1},{3,2},{5,4},{6,5},{7,6},{9,8},{10,9},{11,10},{13,12},{... | collective-permute-start | bytes 2359304 | tf_op jit(solution)/shard_map/ppermute | solution.py:128

commit v5 on v4

--- a/solution.py
+++ b/solution.py
@@ -63,23 +63,41 @@
     )(filter_off, ext)
 
 
-def scatter_kernel(count, cell_ref, scale_ref, rows_ref, out_ref):
-    out_ref[...] = jnp.zeros(out_ref.shape, jnp.float32)
+def scatter_kernel(lanes, shots, tr_dev, base, cell_ref, scale_ref, rows_ref, out_ref, *accs):
+    segments = out_ref.shape[0]
+    span = accs[0].shape[0]
+    for acc in accs:
+        acc[...] = jnp.zeros(acc.shape, jnp.float32)
 
-    def step(r, carry):
-        x = cell_ref[r]
-        out_ref[pl.ds(x, 1), :] += rows_ref[pl.ds(r, 1), :] * scale_ref[r]
+    def step(i, carry):
+        for k, acc in enumerate(accs):
+            r = i * lanes + k
+            x = cell_ref[r] - base
+            src = r // tr_dev
+            row = rows_ref[src, pl.ds(r - src * tr_dev, 1), :]
+            acc[pl.ds(x, 1), :] += row * scale_ref[r]
         return carry
 
-    lax.fori_loop(0, count, step, 0, unroll=8)
+    lax.fori_loop(0, shots * tr_dev // lanes, step, 0, unroll=2)
+    total = accs[0][...]
+    for acc in accs[1:]:
+        total = total + acc[...]
+    out_ref[pl.ds(base, span), :] = total
+    out_ref[pl.ds(0, base), :] = jnp.zeros((base, out_ref.shape[1]), jnp.float32)
+    tail = segments - base - span
+    out_ref[pl.ds(base + span, tail), :] = jnp.zeros((tail, out_ref.shape[1]), jnp.float32)
 
 
-def stack_rows(rows, cells, scale, segments):
-    count, width = rows.shape
-    if width % 128:
+def stack_rows(received, cells, scale, base, span, segments):
+    shots, _, width = received.shape
+    count = cells.shape[0]
+    tr_dev = count // shots
+    lanes = 4
+    if width % 128 or count % lanes or base % 8 or span % 8:
+        rows = received[:, :tr_dev].reshape(count, width)
         return jax.ops.segment_sum(rows * scale[:, None], cells, num_segments=segments)
     return pl.pallas_call(
-        functools.partial(scatter_kernel, count),
+        functools.partial(scatter_kernel, lanes, shots, tr_dev, base),
         in_specs=[
             pl.BlockSpec(memory_space=pltpu.SMEM),
             pl.BlockSpec(memory_space=pltpu.SMEM),
@@ -87,7 +105,9 @@
         ],
         out_specs=pl.BlockSpec(memory_space=pltpu.VMEM),
         out_shape=jax.ShapeDtypeStruct((segments, width), jnp.float32),
-    )(cells, scale, rows)
+        scratch_shapes=[pltpu.VMEM((span, width), jnp.float32) for _ in range(lanes)],
+        compiler_params=pltpu.CompilerParams(vmem_limit_bytes=60 * 1024 * 1024),
+    )(cells, scale, received)
 
 
 def body(traces, cmp_bin, offset_class, bin_rank, filter_off, filter_time):
@@ -112,13 +132,12 @@
     outgoing = jnp.transpose(filtered.reshape(tr_dev, shots, window), (1, 0, 2))
     outgoing = jnp.concatenate([outgoing, labels], axis=1)
     received = lax.all_to_all(outgoing, "shot", 0, 0, tiled=True)
-    rows = received[:, :tr_dev].reshape(shots * tr_dev, window)
     cells = received[:, tr_dev:].reshape(shots, label_rows * window)[:, :tr_dev]
     cells = cells.reshape(shots * tr_dev).astype(jnp.int32)
 
     fold = jnp.sum((cells[:, None] == cells[None, :]).astype(jnp.float32), axis=1)
     scale = 1.0 / jnp.maximum(fold, 1.0)
-    stacked = stack_rows(rows, cells, scale, ext_classes * bin_count)
+    stacked = stack_rows(received, cells, scale, reach * bin_count, off_dev * bin_count, ext_classes * bin_count)
     stacked = stacked.reshape(ext_classes, bin_count, window)
 
     ends = off_count - 1

time: 110 us -> 121 us (1.10)
  Pallas kernels: 21.2 us -> 33.4 us
  local copies, waits for them, and re-layouts: 8.88 us -> 7.37 us
    pallas_call x1, Pallas kernels: 14.3 us -> 26.4 us  [stack_rows(): pl.pallas_call(functools.partial(scatter_kernel, lanes, shots, tr_dev, ba...]
    slice x1 -> x0, local copies, waits for them, and re-layouts: 1.53 us -> none  [body(): rows = received[:, :tr_dev].reshape(shots * tr_dev, window)]
where the time goes in v5:
time: 121 us
  blocking collectives  55.6 us (46%)
  Pallas kernels  33.4 us (28%)
  waiting for transfers between devices  10.4 us (9%)
  local copies, waits for them, and re-layouts  7.37 us (6%)
  starting transfers between devices  6.75 us (6%)
  matrix products  3.55 us (3%)
  other arithmetic  3.49 us (3%)
    all_to_all x1, blocking collectives, body(): received = lax.all_to_all(outgoing, 'shot', 0, 0, tiled=True)  55.6 us
    pallas_call x1, Pallas kernels, stack_rows(): pl.pallas_call(functools.partial(scatter_kernel, lanes, shots, tr_dev, ba...  26.4 us
    ppermute x1, waiting for transfers between devices, body(): before = lax.ppermute(tail, 'off', [(i, i + 1) for i in range(ends)])  6.98 us
    pallas_call x1, Pallas kernels, offset_mix(): pl.pallas_call(functools.partial(mix_kernel, taps, count), grid=(rows //...  6.94 us
    ppermute x1, starting transfers between devices, body(): before = lax.ppermute(tail, 'off', [(i, i + 1) for i in range(ends)])  4.83 us
    dot_general x1, matrix products, block_filter(): jnp.einsum('...ki,io->...ko', extended, table, precision=lax.Precision.HI...  3.55 us
    ppermute x1, waiting for transfers between devices, body(): after = lax.ppermute(head, 'off', [(i + 1, i) for i in range(ends)])  3.47 us
  transfers between devices with their start and end apart: 2, of which 2 were waited for; matrix products, arithmetic and copies ran while one was open for 1% of the time, Pallas kernels for 0%

profile of v5, /device:TPU:1, one launch (start us, length us, event | category | flops | bytes accessed | tf_op | source)
XLA Modules:
  0.0 120.7 jit_solution(13534607942886304332)
XLA Ops:
  0.0 0.0 copy-start.5
  0.0 1.9 %copy.10 = f32[256,2048]{0,1:T(8,128)S(1)} copy(f32[256,2048]{1,0:T(8,128)} %param.6) | data formatting | bytes 4194304 | tf_op args[0]
  1.9 0.1 fusion.13
  2.1 0.0 copy-done.5
  2.1 0.8 select_reduce_fusion
  2.8 3.6 %fusion = f32[256,16,128]{0,2,1:T(8,128)} fusion(f32[256,15,32]{0,2,1:T(8,128)S(1)} %get-tuple-element.8, f32[256,15,32]{0,2,1:T(8,128)S(1)} %get-tuple-element.7, f32[256,16,128]{0,2,1:T(8,128)S(1)} %bitcast.13, f32[192,128]{1,0:T(8,128)S(1)} %select_reduce_fusion), kind=kOutput, calls=%fused_computation.4 | convolution fusion | flops 1212678144 | bytes 5275648 | tf_op jit(solution)/shard_map/...ki,io->...ko/dot_general | solution.py:33
  6.4 0.0 copy-start.2
  6.4 0.0 copy-start.3
  6.4 0.0 copy-start.4
  6.4 2.0 %copy.11 = f32[256,8,256]{2,0,1:T(8,128)S(1)} copy(f32[256,8,256]{0,2,1:T(8,128)} %bitcast.14) | data formatting | bytes 4194304 | tf_op jit(solution)/shard_map/reshape;reshape | solution.py:132
  8.4 0.0 copy-done.2
  8.4 0.0 copy-done.3
  8.4 0.2 select_reduce_fusion.1
  8.6 0.0 copy-done.4
  8.6 0.1 pad_maximum_fusion
  8.7 55.6 %all_to_all.5.rows_ref = f32[8,257,256]{2,1,0:T(8,128)S(1)} all-to-all(f32[8,257,256]{2,1,0:T(8,128)S(1)} %pad_maximum_fusion), channel_id=1, replica_groups=mesh['shot'=8,'off'=4] {'shot'}, dimensions={0} | all-to-all | bytes 4210688 | tf_op jit(solution)/shard_map/all_to_all | solution.py:134
  64.3 0.0 copy-start
  64.3 0.0 copy-start.1
  64.4 1.8 %convert_reduce_fusion = f32[2048]{0:T(1024)S(1)} fusion(s32[2048]{0:T(1024)S(1)} %bitcast.17), kind=kLoop, calls=%fused_computation | loop fusion | flops 12580864 | bytes 16384 | tf_op jit(solution)/shard_map/reduce_sum | solution.py:138
  66.1 0.6 maximum_divide_fusion.scale_ref
  66.7 0.0 copy-done
  66.7 0.0 copy-done.1
  66.7 26.4 %shard_map.64 = f32[6656,256]{1,0:T(8,128)} custom-call(s32[2048]{0:T(1024)} %bitcast.18, f32[2048]{0:T(1024)} %maximum_divide_fusion.scale_ref, f32[8,257,256]{2,1,0:T(8,128)} %copy-done), custom_call_target="tpu_custom_call" | custom-call | tf_op jit(solution)/shard_map/pallas_call | solution.py:99
  93.2 1.5 %fusion.12 = (f32[768,256]{1,0:T(8,128)S(1)}, f32[768,256]{1,0:T(8,128)S(1)}) fusion(f32[6656,256]{1,0:T(8,128)} %shard_map.64), kind=kLoop, calls=%fused_computation.28 | loop fusion | bytes 3145728 | tf_op jit(solution)/shard_map/slice | solution.py:144
  94.6 4.8 %collective-permute-start = (f32[3,256,256]{2,1,0:T(8,128)S(1)}, f32[3,256,256]{2,1,0:T(8,128)S(1)}, u32[]{:S(2)}, u32[]{:S(2)}) collective-permute-start(f32[3,256,256]{2,1,0:T(8,128)S(1)} %bitcast.16), channel_id=1, source_target_pairs={{0,1},{1,2},{2,3},{4,5},{5,6},{6,7},{8,9},{9,10},{10,11},{12,13},{... | collective-permute-start | bytes 2359304 | tf_op jit(solution)/shard_map/ppermute | solution.py:146
  99.5 1.9 %collective-permute-start.1 = (f32[3,256,256]{2,1,0:T(8,128)S(1)}, f32[3,256,256]{2,1,0:T(8,128)S(1)}, u32[]{:S(2)}, u32[]{:S(2)}) collective-permute-start(f32[3,256,256]{2,1,0:T(8,128)S(1)} %bitcast.15), channel_id=1, source_target_pairs={{1,0},{2,1},{3,2},{5,4},{6,5},{7,6},{9,8},{10,9},{11,10},{13,12},{... | collective-permute-start | bytes 2359304 | tf_op jit(solution)/shard_map/ppermute | solution.py:147
  101.4 7.0 %collective-permute-done = f32[3,256,256]{2,1,0:T(8,128)S(1)} collective-permute-done((f32[3,256,256]{2,1,0:T(8,128)S(1)}, f32[3,256,256]{2,1,0:T(8,128)S(1)}, u32[]{:S(2)}, u32[]{:S(2)}) %collective-permute-start) | collective-permute-done | bytes 786464 | tf_op jit(solution)/shard_map/ppermute | solution.py:146
  108.4 0.9 constant_dynamic-update-slice_fusion.1
  109.3 3.5 %collective-permute-done.1 = f32[3,256,256]{2,1,0:T(8,128)S(1)} collective-permute-done((f32[3,256,256]{2,1,0:T(8,128)S(1)}, f32[3,256,256]{2,1,0:T(8,128)S(1)}, u32[]{:S(2)}, u32[]{:S(2)}) %collective-permute-start.1) | collective-permute-done | bytes 786464 | tf_op jit(solution)/shard_map/ppermute | solution.py:147
  112.8 1.0 constant_dynamic-update-slice_fusion.ext_ref
  113.7 6.9 %shard_map.65 = f32[20,256,256]{2,1,0:T(8,128)} custom-call(f32[7]{0:T(128)} %filter_ref.1, f32[26,256,256]{2,1,0:T(8,128)} %constant_dynamic-update-slice_fusion.ext_ref), custom_call_target="tpu_custom_call" | custom-call | tf_op jit(solution)/shard_map/pallas_call | solution.py:54
  (4 shorter events, 0.0 us)
Async XLA Ops:
  0.0 2.1 %copy-start.5 = (f32[65]{0:T(128)S(1)}, f32[65]{0:T(128)}, u32[]{:S(2)}) copy-start(f32[65]{0:T(128)} %param.11) | copy-start | bytes 784
  6.4 2.0 %copy-start.2 = (s32[256]{0:T(256)S(1)}, s32[256]{0:T(256)}, u32[]{:S(2)}) copy-start(s32[256]{0:T(256)} %param.9) | copy-start | bytes 3076
  6.4 2.0 %copy-start.3 = (s32[256]{0:T(256)S(1)}, s32[256]{0:T(256)}, u32[]{:S(2)}) copy-start(s32[256]{0:T(256)} %param.7) | copy-start | bytes 3076
  6.4 2.2 %copy-start.4 = (s32[256]{0:T(256)S(1)}, s32[256]{0:T(256)}, u32[]{:S(2)}) copy-start(s32[256]{0:T(256)} %param.8) | copy-start | bytes 3076
  64.3 2.4 %copy-start = (f32[8,257,256]{2,1,0:T(8,128)}, f32[8,257,256]{2,1,0:T(8,128)S(1)}, u32[]{:S(2)}) copy-start(f32[8,257,256]{2,1,0:T(8,128)S(1)} %all_to_all.5.rows_ref) | copy-start | bytes 6316036
  64.3 2.4 %copy-start.1 = (s32[8,1,256]{2,1,0:T(1,128)}, s32[8,1,256]{2,1,0:T(1,128)S(1)}, u32[]{:S(2)}) copy-start(s32[8,1,256]{2,1,0:T(1,128)S(1)} %slice_convert_fusion) | copy-start | bytes 24580
  94.6 13.8 %collective-permute-start = (f32[3,256,256]{2,1,0:T(8,128)S(1)}, f32[3,256,256]{2,1,0:T(8,128)S(1)}, u32[]{:S(2)}, u32[]{:S(2)}) collective-permute-start(f32[3,256,256]{2,1,0:T(8,128)S(1)} %bitcast.16), channel_id=1, source_target_pairs={{0,1},{1,2},{2,3},{4,5},{5,6},{6,7},{8,9},{9,10},{10,11},{12,13},{... | collective-permute-start | bytes 2359304 | tf_op jit(solution)/shard_map/ppermute | solution.py:146
  99.5 13.3 %collective-permute-start.1 = (f32[3,256,256]{2,1,0:T(8,128)S(1)}, f32[3,256,256]{2,1,0:T(8,128)S(1)}, u32[]{:S(2)}, u32[]{:S(2)}) collective-permute-start(f32[3,256,256]{2,1,0:T(8,128)S(1)} %bitcast.15), channel_id=1, source_target_pairs={{1,0},{2,1},{3,2},{5,4},{6,5},{7,6},{9,8},{10,9},{11,10},{13,12},{... | collective-permute-start | bytes 2359304 | tf_op jit(solution)/shard_map/ppermute | solution.py:147

commit v6 on v4

--- a/solution.py
+++ b/solution.py
@@ -66,17 +66,20 @@
 def scatter_kernel(count, cell_ref, scale_ref, rows_ref, out_ref):
     out_ref[...] = jnp.zeros(out_ref.shape, jnp.float32)
 
-    def step(r, carry):
-        x = cell_ref[r]
-        out_ref[pl.ds(x, 1), :] += rows_ref[pl.ds(r, 1), :] * scale_ref[r]
+    def step(i, carry):
+        start = pl.multiple_of(i * 8, 8)
+        tile = rows_ref[pl.ds(start, 8), :]
+        for k in range(8):
+            x = cell_ref[start + k]
+            out_ref[pl.ds(x, 1), :] += tile[k : k + 1, :] * scale_ref[start + k]
         return carry
 
-    lax.fori_loop(0, count, step, 0, unroll=8)
+    lax.fori_loop(0, count // 8, step, 0)
 
 
 def stack_rows(rows, cells, scale, segments):
     count, width = rows.shape
-    if width % 128:
+    if width % 128 or count % 8:
         return jax.ops.segment_sum(rows * scale[:, None], cells, num_segments=segments)
     return pl.pallas_call(
         functools.partial(scatter_kernel, count),

time: 110 us -> 109 us (level)
  Pallas kernels: 21.2 us -> 19.9 us
    pallas_call x1, Pallas kernels: 14.3 us -> 12.9 us  [stack_rows(): pl.pallas_call(functools.partial(scatter_kernel, count), in_specs=[pl.Blo...]
where the time goes in v6:
time: 109 us
  blocking collectives  55.6 us (51%)
  Pallas kernels  19.9 us (18%)
  waiting for transfers between devices  10.4 us (10%)
  local copies, waits for them, and re-layouts  8.88 us (8%)
  starting transfers between devices  6.75 us (6%)
  matrix products  3.55 us (3%)
  other arithmetic  3.49 us (3%)
    all_to_all x1, blocking collectives, body(): received = lax.all_to_all(outgoing, 'shot', 0, 0, tiled=True)  55.6 us
    pallas_call x1, Pallas kernels, stack_rows(): pl.pallas_call(functools.partial(scatter_kernel, count), in_specs=[pl.Blo...  12.9 us
    ppermute x1, waiting for transfers between devices, body(): before = lax.ppermute(tail, 'off', [(i, i + 1) for i in range(ends)])  6.98 us
    pallas_call x1, Pallas kernels, offset_mix(): pl.pallas_call(functools.partial(mix_kernel, taps, count), grid=(rows //...  6.94 us
    ppermute x1, starting transfers between devices, body(): before = lax.ppermute(tail, 'off', [(i, i + 1) for i in range(ends)])  4.83 us
    dot_general x1, matrix products, block_filter(): jnp.einsum('...ki,io->...ko', extended, table, precision=lax.Precision.HI...  3.55 us
    ppermute x1, waiting for transfers between devices, body(): after = lax.ppermute(head, 'off', [(i + 1, i) for i in range(ends)])  3.46 us
  transfers between devices with their start and end apart: 2, of which 2 were waited for; matrix products, arithmetic and copies ran while one was open for 1% of the time, Pallas kernels for 0%

profile of v6, /device:TPU:1, one launch (start us, length us, event | category | flops | bytes accessed | tf_op | source)
XLA Modules:
  0.0 108.7 jit_solution(15818669329262581243)
XLA Ops:
  0.0 0.0 copy-start.4
  0.0 1.9 %copy.9 = f32[256,2048]{0,1:T(8,128)S(1)} copy(f32[256,2048]{1,0:T(8,128)} %param.6) | data formatting | bytes 4194304 | tf_op args[0]
  1.9 0.1 fusion.13
  2.1 0.0 copy-done.4
  2.1 0.8 select_reduce_fusion
  2.8 3.6 %fusion = f32[256,16,128]{0,2,1:T(8,128)} fusion(f32[256,15,32]{0,2,1:T(8,128)S(1)} %get-tuple-element.8, f32[256,15,32]{0,2,1:T(8,128)S(1)} %get-tuple-element.7, f32[256,16,128]{0,2,1:T(8,128)S(1)} %bitcast.15, f32[192,128]{1,0:T(8,128)S(1)} %select_reduce_fusion), kind=kOutput, calls=%fused_computation.4 | convolution fusion | flops 1212678144 | bytes 5275648 | tf_op jit(solution)/shard_map/...ki,io->...ko/dot_general | solution.py:33
  6.4 0.0 copy-start.1
  6.4 0.0 copy-start.2
  6.4 0.0 copy-start.3
  6.4 2.0 %copy.10 = f32[256,8,256]{2,0,1:T(8,128)S(1)} copy(f32[256,8,256]{0,2,1:T(8,128)} %bitcast.16) | data formatting | bytes 4194304 | tf_op jit(solution)/shard_map/reshape;reshape | solution.py:115
  8.4 0.0 copy-done.1
  8.4 0.0 copy-done.2
  8.4 0.2 select_reduce_fusion.1
  8.6 0.0 copy-done.3
  8.6 0.1 pad_maximum_fusion
  8.7 55.6 %all_to_all.5 = f32[8,257,256]{2,1,0:T(8,128)S(1)} all-to-all(f32[8,257,256]{2,1,0:T(8,128)S(1)} %pad_maximum_fusion), channel_id=1, replica_groups=mesh['shot'=8,'off'=4] {'shot'}, dimensions={0} | all-to-all | bytes 4210688 | tf_op jit(solution)/shard_map/all_to_all | solution.py:117
  64.3 0.0 copy-start
  64.4 1.8 %convert_reduce_fusion = f32[2048]{0:T(1024)S(1)} fusion(s32[2048]{0:T(1024)S(1)} %bitcast.19), kind=kLoop, calls=%fused_computation | loop fusion | flops 12580864 | bytes 16384 | tf_op jit(solution)/shard_map/reduce_sum | solution.py:122
  66.1 0.6 maximum_divide_fusion.scale_ref
  66.7 1.5 %slice.35 = f32[8,256,256]{2,1,0:T(8,128)} slice(f32[8,257,256]{2,1,0:T(8,128)S(1)} %all_to_all.5), slice={[0:8], [0:256], [0:256]} | slice | bytes 4194304 | tf_op jit(solution)/shard_map/slice | solution.py:118
  68.3 0.0 copy-done
  68.3 12.9 %shard_map.64 = f32[6656,256]{1,0:T(8,128)} custom-call(s32[2048]{0:T(1024)} %bitcast.20, f32[2048]{0:T(1024)} %maximum_divide_fusion.scale_ref, f32[2048,256]{1,0:T(8,128)} %bitcast.12), custom_call_target="tpu_custom_call" | custom-call | tf_op jit(solution)/shard_map/pallas_call | solution.py:84
  81.2 1.5 %fusion.12 = (f32[768,256]{1,0:T(8,128)S(1)}, f32[768,256]{1,0:T(8,128)S(1)}) fusion(f32[6656,256]{1,0:T(8,128)} %shard_map.64), kind=kLoop, calls=%fused_computation.28 | loop fusion | bytes 3145728 | tf_op jit(solution)/shard_map/slice | solution.py:128
  82.6 4.8 %collective-permute-start = (f32[3,256,256]{2,1,0:T(8,128)S(1)}, f32[3,256,256]{2,1,0:T(8,128)S(1)}, u32[]{:S(2)}, u32[]{:S(2)}) collective-permute-start(f32[3,256,256]{2,1,0:T(8,128)S(1)} %bitcast.18), channel_id=1, source_target_pairs={{0,1},{1,2},{2,3},{4,5},{5,6},{6,7},{8,9},{9,10},{10,11},{12,13},{... | collective-permute-start | bytes 2359304 | tf_op jit(solution)/shard_map/ppermute | solution.py:130
  87.5 1.9 %collective-permute-start.1 = (f32[3,256,256]{2,1,0:T(8,128)S(1)}, f32[3,256,256]{2,1,0:T(8,128)S(1)}, u32[]{:S(2)}, u32[]{:S(2)}) collective-permute-start(f32[3,256,256]{2,1,0:T(8,128)S(1)} %bitcast.17), channel_id=1, source_target_pairs={{1,0},{2,1},{3,2},{5,4},{6,5},{7,6},{9,8},{10,9},{11,10},{13,12},{... | collective-permute-start | bytes 2359304 | tf_op jit(solution)/shard_map/ppermute | solution.py:131
  89.4 7.0 %collective-permute-done = f32[3,256,256]{2,1,0:T(8,128)S(1)} collective-permute-done((f32[3,256,256]{2,1,0:T(8,128)S(1)}, f32[3,256,256]{2,1,0:T(8,128)S(1)}, u32[]{:S(2)}, u32[]{:S(2)}) %collective-permute-start) | collective-permute-done | bytes 786464 | tf_op jit(solution)/shard_map/ppermute | solution.py:130
  96.4 0.9 constant_dynamic-update-slice_fusion.1
  97.3 3.5 %collective-permute-done.1 = f32[3,256,256]{2,1,0:T(8,128)S(1)} collective-permute-done((f32[3,256,256]{2,1,0:T(8,128)S(1)}, f32[3,256,256]{2,1,0:T(8,128)S(1)}, u32[]{:S(2)}, u32[]{:S(2)}) %collective-permute-start.1) | collective-permute-done | bytes 786464 | tf_op jit(solution)/shard_map/ppermute | solution.py:131
  100.8 0.9 constant_dynamic-update-slice_fusion.ext_ref
  101.7 6.9 %shard_map.65 = f32[20,256,256]{2,1,0:T(8,128)} custom-call(f32[7]{0:T(128)} %filter_ref.1, f32[26,256,256]{2,1,0:T(8,128)} %constant_dynamic-update-slice_fusion.ext_ref), custom_call_target="tpu_custom_call" | custom-call | tf_op jit(solution)/shard_map/pallas_call | solution.py:54
  (4 shorter events, 0.0 us)
Async XLA Ops:
  0.0 2.1 %copy-start.4 = (f32[65]{0:T(128)S(1)}, f32[65]{0:T(128)}, u32[]{:S(2)}) copy-start(f32[65]{0:T(128)} %param.11) | copy-start | bytes 784
  6.4 2.0 %copy-start.1 = (s32[256]{0:T(256)S(1)}, s32[256]{0:T(256)}, u32[]{:S(2)}) copy-start(s32[256]{0:T(256)} %param.9) | copy-start | bytes 3076
  6.4 2.0 %copy-start.2 = (s32[256]{0:T(256)S(1)}, s32[256]{0:T(256)}, u32[]{:S(2)}) copy-start(s32[256]{0:T(256)} %param.7) | copy-start | bytes 3076
  6.4 2.2 %copy-start.3 = (s32[256]{0:T(256)S(1)}, s32[256]{0:T(256)}, u32[]{:S(2)}) copy-start(s32[256]{0:T(256)} %param.8) | copy-start | bytes 3076
  64.3 3.9 %copy-start = (s32[8,1,256]{2,1,0:T(1,128)}, s32[8,1,256]{2,1,0:T(1,128)S(1)}, u32[]{:S(2)}) copy-start(s32[8,1,256]{2,1,0:T(1,128)S(1)} %slice_convert_fusion) | copy-start | bytes 24580
  82.6 13.8 %collective-permute-start = (f32[3,256,256]{2,1,0:T(8,128)S(1)}, f32[3,256,256]{2,1,0:T(8,128)S(1)}, u32[]{:S(2)}, u32[]{:S(2)}) collective-permute-start(f32[3,256,256]{2,1,0:T(8,128)S(1)} %bitcast.18), channel_id=1, source_target_pairs={{0,1},{1,2},{2,3},{4,5},{5,6},{6,7},{8,9},{9,10},{10,11},{12,13},{... | collective-permute-start | bytes 2359304 | tf_op jit(solution)/shard_map/ppermute | solution.py:130
  87.5 13.3 %collective-permute-start.1 = (f32[3,256,256]{2,1,0:T(8,128)S(1)}, f32[3,256,256]{2,1,0:T(8,128)S(1)}, u32[]{:S(2)}, u32[]{:S(2)}) collective-permute-start(f32[3,256,256]{2,1,0:T(8,128)S(1)} %bitcast.17), channel_id=1, source_target_pairs={{1,0},{2,1},{3,2},{5,4},{6,5},{7,6},{9,8},{10,9},{11,10},{13,12},{... | collective-permute-start | bytes 2359304 | tf_op jit(solution)/shard_map/ppermute | solution.py:131

commit v7 on v6

--- a/solution.py
+++ b/solution.py
@@ -34,33 +34,44 @@
     return result.reshape(leading + (samples,))
 
 
-def mix_kernel(taps, count, filter_ref, ext_ref, out_ref):
+def mix_kernel(taps, count, reach, filter_ref, before_ref, own_ref, after_ref, out_ref):
+    def plane(e):
+        if e < reach:
+            return before_ref[e]
+        if e < reach + count:
+            return own_ref[e - reach]
+        return after_ref[e - reach - count]
+
     for c in range(count):
-        acc = filter_ref[0] * ext_ref[c]
+        acc = filter_ref[0] * plane(c)
         for k in range(1, taps):
-            acc = acc + filter_ref[k] * ext_ref[c + k]
+            acc = acc + filter_ref[k] * plane(c + k)
         out_ref[c] = acc.T
 
 
-def offset_mix(ext, filter_off, count):
+def offset_mix(before, own, after, filter_off):
     taps = filter_off.shape[0]
-    classes, rows, cols = ext.shape
+    count, rows, cols = own.shape
+    reach = before.shape[0]
     if rows % 128 or cols % 128:
+        ext = jnp.concatenate([before, own, after], axis=0)
         mixed = filter_off[0] * ext[0:count]
         for k in range(1, taps):
             mixed = mixed + filter_off[k] * ext[k : k + count]
         return jnp.transpose(mixed, (0, 2, 1))
     tile = 128
     return pl.pallas_call(
-        functools.partial(mix_kernel, taps, count),
+        functools.partial(mix_kernel, taps, count, reach),
         grid=(rows // tile, cols // tile),
         in_specs=[
             pl.BlockSpec(memory_space=pltpu.SMEM),
-            pl.BlockSpec((classes, tile, tile), lambda i, j: (0, i, j)),
+            pl.BlockSpec((reach, tile, tile), lambda i, j: (0, i, j)),
+            pl.BlockSpec((count, tile, tile), lambda i, j: (0, i, j)),
+            pl.BlockSpec((reach, tile, tile), lambda i, j: (0, i, j)),
         ],
         out_specs=pl.BlockSpec((count, tile, tile), lambda i, j: (0, j, i)),
         out_shape=jax.ShapeDtypeStruct((count, cols, rows), jnp.float32),
-    )(filter_off, ext)
+    )(filter_off, before, own, after)
 
 
 def scatter_kernel(count, cell_ref, scale_ref, rows_ref, out_ref):
@@ -102,11 +113,10 @@
     tr_dev, samples = traces.shape
     window = samples // shots
     reach = filter_off.shape[0] // 2
-    ext_classes = off_dev + 2 * reach
 
     matches = cmp_bin[:, None] == jnp.arange(bin_count, dtype=jnp.int32)[None, :]
     place = jnp.sum(jnp.where(matches, bin_rank[None, :], 0), axis=1)
-    cell = (offset_class - first_class + reach) * bin_count + place
+    cell = (offset_class - first_class) * bin_count + place
     label_rows = -(-tr_dev // window)
     labels = jnp.pad(cell.astype(jnp.float32), (0, label_rows * window - tr_dev))
     labels = jnp.broadcast_to(labels.reshape(1, label_rows, window), (shots, label_rows, window))
@@ -121,17 +131,15 @@
 
     fold = jnp.sum((cells[:, None] == cells[None, :]).astype(jnp.float32), axis=1)
     scale = 1.0 / jnp.maximum(fold, 1.0)
-    stacked = stack_rows(rows, cells, scale, ext_classes * bin_count)
-    stacked = stacked.reshape(ext_classes, bin_count, window)
+    stacked = stack_rows(rows, cells, scale, off_dev * bin_count)
+    stacked = stacked.reshape(off_dev, bin_count, window)
 
     ends = off_count - 1
-    head = stacked[reach : 2 * reach]
-    tail = stacked[off_dev : off_dev + reach]
+    head = stacked[:reach]
+    tail = stacked[off_dev - reach :]
     before = lax.ppermute(tail, "off", [(i, i + 1) for i in range(ends)])
     after = lax.ppermute(head, "off", [(i + 1, i) for i in range(ends)])
-    ext = lax.dynamic_update_slice_in_dim(stacked, before, 0, axis=0)
-    ext = lax.dynamic_update_slice_in_dim(ext, after, off_dev + reach, axis=0)
-    return offset_mix(ext, filter_off, off_dev)
+    return offset_mix(before, stacked, after, filter_off)
 
 
 def solution(mesh):

time: 109 us -> 108 us (level)
    dynamic_update_slice x2 -> x0, local copies, waits for them, and re-layouts: 1.88 us -> none  [the longest x1 0.94 us: body(): ext = lax.dynamic_update_slice_in_dim(ext, after, off_dev + reach, axis=0)]
    unnamed x11 -> x15, local copies, waits for them, and re-layouts: 1.94 us -> 2.85 us
  transfers between devices with their start and end apart: 2 -> 2, of which waited for: 2 -> 2; matrix products, arithmetic and copies ran while one was open for 1% -> 0% of each run, Pallas kernels for 0% -> 0%
where the time goes in v7:
time: 108 us
  blocking collectives  55.6 us (51%)
  Pallas kernels  19.2 us (18%)
  waiting for transfers between devices  11.4 us (11%)
  local copies, waits for them, and re-layouts  7.9 us (7%)
  starting transfers between devices  6.75 us (6%)
  matrix products  3.55 us (3%)
  other arithmetic  3.49 us (3%)
    all_to_all x1, blocking collectives, body(): received = lax.all_to_all(outgoing, 'shot', 0, 0, tiled=True)  55.6 us
    pallas_call x1, Pallas kernels, stack_rows(): pl.pallas_call(functools.partial(scatter_kernel, count), in_specs=[pl.Blo...  12.3 us
    ppermute x1, waiting for transfers between devices, body(): before = lax.ppermute(tail, 'off', [(i, i + 1) for i in range(ends)])  6.98 us
    pallas_call x1, Pallas kernels, offset_mix(): pl.pallas_call(functools.partial(mix_kernel, taps, count, reach), grid=(r...  6.89 us
    ppermute x1, starting transfers between devices, body(): before = lax.ppermute(tail, 'off', [(i, i + 1) for i in range(ends)])  4.83 us
    ppermute x1, waiting for transfers between devices, body(): after = lax.ppermute(head, 'off', [(i + 1, i) for i in range(ends)])  4.39 us
    dot_general x1, matrix products, block_filter(): jnp.einsum('...ki,io->...ko', extended, table, precision=lax.Precision.HI...  3.55 us
    unnamed x15, local copies, waits for them, and re-layouts  2.85 us
  transfers between devices with their start and end apart: 2, of which 2 were waited for; matrix products, arithmetic and copies ran while one was open for 0% of the time, Pallas kernels for 0%

profile of v7, /device:TPU:1, one launch (start us, length us, event | category | flops | bytes accessed | tf_op | source)
XLA Modules:
  0.0 108.0 jit_solution(11358387295263661156)
XLA Ops:
  0.0 0.0 copy-start.6
  0.0 1.9 %copy.9 = f32[256,2048]{0,1:T(8,128)S(1)} copy(f32[256,2048]{1,0:T(8,128)} %param.6) | data formatting | bytes 4194304 | tf_op args[0]
  1.9 0.1 fusion.13
  2.1 0.0 copy-done.6
  2.1 0.8 select_reduce_fusion
  2.8 3.6 %fusion = f32[256,16,128]{0,2,1:T(8,128)} fusion(f32[256,15,32]{0,2,1:T(8,128)S(1)} %get-tuple-element.8, f32[256,15,32]{0,2,1:T(8,128)S(1)} %get-tuple-element.7, f32[256,16,128]{0,2,1:T(8,128)S(1)} %bitcast.15, f32[192,128]{1,0:T(8,128)S(1)} %select_reduce_fusion), kind=kOutput, calls=%fused_computation.4 | convolution fusion | flops 1212678144 | bytes 5275648 | tf_op jit(solution)/shard_map/...ki,io->...ko/dot_general | solution.py:33
  6.4 0.0 copy-start.3
  6.4 0.0 copy-start.4
  6.4 0.0 copy-start.5
  6.4 2.0 %copy.10 = f32[256,8,256]{2,0,1:T(8,128)S(1)} copy(f32[256,8,256]{0,2,1:T(8,128)} %bitcast.16) | data formatting | bytes 4194304 | tf_op jit(solution)/shard_map/reshape;reshape | solution.py:125
  8.4 0.0 copy-done.3
  8.4 0.0 copy-done.4
  8.4 0.2 select_reduce_fusion.1
  8.6 0.0 copy-done.5
  8.6 0.1 pad_maximum_fusion
  8.7 55.6 %all_to_all.5 = f32[8,257,256]{2,1,0:T(8,128)S(1)} all-to-all(f32[8,257,256]{2,1,0:T(8,128)S(1)} %pad_maximum_fusion), channel_id=1, replica_groups=mesh['shot'=8,'off'=4] {'shot'}, dimensions={0} | all-to-all | bytes 4210688 | tf_op jit(solution)/shard_map/all_to_all | solution.py:127
  64.3 0.0 copy-start.2
  64.4 1.8 %convert_reduce_fusion = f32[2048]{0:T(1024)S(1)} fusion(s32[2048]{0:T(1024)S(1)} %bitcast.19), kind=kLoop, calls=%fused_computation | loop fusion | flops 12580864 | bytes 16384 | tf_op jit(solution)/shard_map/reduce_sum | solution.py:132
  66.1 0.6 maximum_divide_fusion.scale_ref
  66.7 1.5 %slice.35 = f32[8,256,256]{2,1,0:T(8,128)} slice(f32[8,257,256]{2,1,0:T(8,128)S(1)} %all_to_all.5), slice={[0:8], [0:256], [0:256]} | slice | bytes 4194304 | tf_op jit(solution)/shard_map/slice | solution.py:128
  68.3 0.0 copy-done.2
  68.3 12.3 %shard_map.64 = f32[5120,256]{1,0:T(8,128)} custom-call(s32[2048]{0:T(1024)} %bitcast.20, f32[2048]{0:T(1024)} %maximum_divide_fusion.scale_ref, f32[2048,256]{1,0:T(8,128)} %bitcast.12), custom_call_target="tpu_custom_call" | custom-call | tf_op jit(solution)/shard_map/pallas_call | solution.py:95
  80.6 1.5 %fusion.12 = (f32[768,256]{1,0:T(8,128)S(1)}, f32[768,256]{1,0:T(8,128)S(1)}) fusion(f32[5120,256]{1,0:T(8,128)} %shard_map.64), kind=kLoop, calls=%fused_computation.26 | loop fusion | bytes 3145728 | tf_op jit(solution)/shard_map/slice | solution.py:138
  82.1 4.8 %collective-permute-start = (f32[3,256,256]{2,1,0:T(8,128)S(1)}, f32[3,256,256]{2,1,0:T(8,128)S(1)}, u32[]{:S(2)}, u32[]{:S(2)}) collective-permute-start(f32[3,256,256]{2,1,0:T(8,128)S(1)} %bitcast.18), channel_id=1, source_target_pairs={{0,1},{1,2},{2,3},{4,5},{5,6},{6,7},{8,9},{9,10},{10,11},{12,13},{... | collective-permute-start | bytes 2359304 | tf_op jit(solution)/shard_map/ppermute | solution.py:140
  86.9 1.9 %collective-permute-start.1 = (f32[3,256,256]{2,1,0:T(8,128)S(1)}, f32[3,256,256]{2,1,0:T(8,128)S(1)}, u32[]{:S(2)}, u32[]{:S(2)}) collective-permute-start(f32[3,256,256]{2,1,0:T(8,128)S(1)} %bitcast.17), channel_id=1, source_target_pairs={{1,0},{2,1},{3,2},{5,4},{6,5},{7,6},{9,8},{10,9},{11,10},{13,12},{... | collective-permute-start | bytes 2359304 | tf_op jit(solution)/shard_map/ppermute | solution.py:141
  88.8 7.0 %collective-permute-done.before_ref = f32[3,256,256]{2,1,0:T(8,128)S(1)} collective-permute-done((f32[3,256,256]{2,1,0:T(8,128)S(1)}, f32[3,256,256]{2,1,0:T(8,128)S(1)}, u32[]{:S(2)}, u32[]{:S(2)}) %collective-permute-start) | collective-permute-done | bytes 786464 | tf_op jit(solution)/shard_map/ppermute | solution.py:140
  95.8 0.0 copy-start
  95.8 4.4 %collective-permute-done.1.after_ref = f32[3,256,256]{2,1,0:T(8,128)S(1)} collective-permute-done((f32[3,256,256]{2,1,0:T(8,128)S(1)}, f32[3,256,256]{2,1,0:T(8,128)S(1)}, u32[]{:S(2)}, u32[]{:S(2)}) %collective-permute-start.1) | collective-permute-done | bytes 786464 | tf_op jit(solution)/shard_map/ppermute | solution.py:141
  100.2 0.0 copy-start.1
  100.2 0.0 copy-done
  100.2 0.9 copy-done.1
  101.1 6.9 %shard_map.65 = f32[20,256,256]{2,1,0:T(8,128)} custom-call(f32[7]{0:T(128)} %filter_ref.1, f32[3,256,256]{2,1,0:T(8,128)} %copy-done, f32[20,256,256]{2,1,0:T(8,128)} %bitcast.11, f32[3,256,256]{2,1,0:T(8,128)} %copy-done.1), custom_call_target="tpu_custom_call" | custom-call | tf_op jit(solution)/shard_map/pallas_call | solution.py:63
  (4 shorter events, 0.0 us)
Async XLA Ops:
  0.0 2.1 %copy-start.6 = (f32[65]{0:T(128)S(1)}, f32[65]{0:T(128)}, u32[]{:S(2)}) copy-start(f32[65]{0:T(128)} %param.11) | copy-start | bytes 784
  6.4 2.0 %copy-start.3 = (s32[256]{0:T(256)S(1)}, s32[256]{0:T(256)}, u32[]{:S(2)}) copy-start(s32[256]{0:T(256)} %param.9) | copy-start | bytes 3076
  6.4 2.0 %copy-start.4 = (s32[256]{0:T(256)S(1)}, s32[256]{0:T(256)}, u32[]{:S(2)}) copy-start(s32[256]{0:T(256)} %param.7) | copy-start | bytes 3076
  6.4 2.2 %copy-start.5 = (s32[256]{0:T(256)S(1)}, s32[256]{0:T(256)}, u32[]{:S(2)}) copy-start(s32[256]{0:T(256)} %param.8) | copy-start | bytes 3076
  64.3 3.9 %copy-start.2 = (s32[8,1,256]{2,1,0:T(1,128)}, s32[8,1,256]{2,1,0:T(1,128)S(1)}, u32[]{:S(2)}) copy-start(s32[8,1,256]{2,1,0:T(1,128)S(1)} %slice_convert_fusion) | copy-start | bytes 24580
  82.1 13.8 %collective-permute-start = (f32[3,256,256]{2,1,0:T(8,128)S(1)}, f32[3,256,256]{2,1,0:T(8,128)S(1)}, u32[]{:S(2)}, u32[]{:S(2)}) collective-permute-start(f32[3,256,256]{2,1,0:T(8,128)S(1)} %bitcast.18), channel_id=1, source_target_pairs={{0,1},{1,2},{2,3},{4,5},{5,6},{6,7},{8,9},{9,10},{10,11},{12,13},{... | collective-permute-start | bytes 2359304 | tf_op jit(solution)/shard_map/ppermute | solution.py:140
  86.9 13.3 %collective-permute-start.1 = (f32[3,256,256]{2,1,0:T(8,128)S(1)}, f32[3,256,256]{2,1,0:T(8,128)S(1)}, u32[]{:S(2)}, u32[]{:S(2)}) collective-permute-start(f32[3,256,256]{2,1,0:T(8,128)S(1)} %bitcast.17), channel_id=1, source_target_pairs={{1,0},{2,1},{3,2},{5,4},{6,5},{7,6},{9,8},{10,9},{11,10},{13,12},{... | collective-permute-start | bytes 2359304 | tf_op jit(solution)/shard_map/ppermute | solution.py:141
  95.8 4.4 %copy-start = (f32[3,256,256]{2,1,0:T(8,128)}, f32[3,256,256]{2,1,0:T(8,128)S(1)}, u32[]{:S(2)}) copy-start(f32[3,256,256]{2,1,0:T(8,128)S(1)} %collective-permute-done.before_ref) | copy-start | bytes 2359300
  100.2 0.9 copy-start.1

commit v8 on v7

--- a/solution.py
+++ b/solution.py
@@ -34,7 +34,7 @@
     return result.reshape(leading + (samples,))
 
 
-def mix_kernel(taps, count, reach, filter_ref, before_ref, own_ref, after_ref, out_ref):
+def mix_class(taps, count, reach, filter_ref, before_ref, own_ref, after_ref, c):
     def plane(e):
         if e < reach:
             return before_ref[e]
@@ -42,36 +42,62 @@
             return own_ref[e - reach]
         return after_ref[e - reach - count]
 
-    for c in range(count):
-        acc = filter_ref[0] * plane(c)
-        for k in range(1, taps):
-            acc = acc + filter_ref[k] * plane(c + k)
-        out_ref[c] = acc.T
+    acc = filter_ref[0] * plane(c)
+    for k in range(1, taps):
+        acc = acc + filter_ref[k] * plane(c + k)
+    return acc.T
+
+
+def inner_kernel(taps, count, reach, filter_ref, own_ref, out_ref):
+    for c in range(reach, count - reach):
+        out_ref[c] = mix_class(taps, count, reach, filter_ref, None, own_ref, None, c)
+
+
+def edge_kernel(taps, count, reach, filter_ref, before_ref, own_ref, after_ref, _, out_ref):
+    step = pl.program_id(2)
+    edges = list(range(reach)) + list(range(count - reach, count))
+    for slot, c in enumerate(edges):
+        @pl.when(step == slot)
+        def _():
+            out_ref[0] = mix_class(taps, count, reach, filter_ref, before_ref, own_ref, after_ref, c)
 
 
 def offset_mix(before, own, after, filter_off):
     taps = filter_off.shape[0]
     count, rows, cols = own.shape
     reach = before.shape[0]
-    if rows % 128 or cols % 128:
+    if rows % 128 or cols % 128 or count < 2 * reach:
         ext = jnp.concatenate([before, own, after], axis=0)
         mixed = filter_off[0] * ext[0:count]
         for k in range(1, taps):
             mixed = mixed + filter_off[k] * ext[k : k + count]
         return jnp.transpose(mixed, (0, 2, 1))
     tile = 128
-    return pl.pallas_call(
-        functools.partial(mix_kernel, taps, count, reach),
+    inner = pl.pallas_call(
+        functools.partial(inner_kernel, taps, count, reach),
         grid=(rows // tile, cols // tile),
         in_specs=[
             pl.BlockSpec(memory_space=pltpu.SMEM),
-            pl.BlockSpec((reach, tile, tile), lambda i, j: (0, i, j)),
             pl.BlockSpec((count, tile, tile), lambda i, j: (0, i, j)),
-            pl.BlockSpec((reach, tile, tile), lambda i, j: (0, i, j)),
         ],
         out_specs=pl.BlockSpec((count, tile, tile), lambda i, j: (0, j, i)),
         out_shape=jax.ShapeDtypeStruct((count, cols, rows), jnp.float32),
-    )(filter_off, before, own, after)
+    )(filter_off, own)
+    shift = count - 2 * reach
+    return pl.pallas_call(
+        functools.partial(edge_kernel, taps, count, reach),
+        grid=(rows // tile, cols // tile, 2 * reach),
+        in_specs=[
+            pl.BlockSpec(memory_space=pltpu.SMEM),
+            pl.BlockSpec((reach, tile, tile), lambda i, j, e: (0, i, j)),
+            pl.BlockSpec((count, tile, tile), lambda i, j, e: (0, i, j)),
+            pl.BlockSpec((reach, tile, tile), lambda i, j, e: (0, i, j)),
+            pl.BlockSpec(memory_space=pl.ANY),
+        ],
+        out_specs=pl.BlockSpec((1, tile, tile), lambda i, j, e: (e + (e >= reach) * shift, j, i)),
+        out_shape=jax.ShapeDtypeStruct((count, cols, rows), jnp.float32),
+        input_output_aliases={4: 0},
+    )(filter_off, before, own, after, inner)
 
 
 def scatter_kernel(count, cell_ref, scale_ref, rows_ref, out_ref):

time: 108 us -> 115 us (1.065)
  Pallas kernels: 19.2 us -> 32.2 us
  waiting for transfers between devices: 11.4 us -> 5.18 us
    pallas_call x1 -> x2, Pallas kernels: 6.89 us -> 19.8 us  [the longest x1 13.6 us: offset_mix(): pl.pallas_call(functools.partial(edge_kernel, taps, count, reach), grid=(...]
    ppermute x1, waiting for transfers between devices: 6.98 us -> 0.79 us  [body(): before = lax.ppermute(tail, 'off', [(i, i + 1) for i in range(ends)])]
  transfers between devices with their start and end apart: 2 -> 2, of which waited for: 2 -> 2; matrix products, arithmetic and copies ran while one was open for 0% -> 0% of each run, Pallas kernels for 0% -> 5%
where the time goes in v8:
time: 115 us
  blocking collectives  55.6 us (48%)
  Pallas kernels  32.2 us (28%)
  local copies, waits for them, and re-layouts  7.91 us (7%)
  starting transfers between devices  6.75 us (6%)
  waiting for transfers between devices  5.18 us (5%)
  matrix products  3.55 us (3%)
  other arithmetic  3.49 us (3%)
    all_to_all x1, blocking collectives, body(): received = lax.all_to_all(outgoing, 'shot', 0, 0, tiled=True)  55.6 us
    pallas_call x1, Pallas kernels, offset_mix(): pl.pallas_call(functools.partial(edge_kernel, taps, count, reach), grid=(...  13.6 us
    pallas_call x1, Pallas kernels, stack_rows(): pl.pallas_call(functools.partial(scatter_kernel, count), in_specs=[pl.Blo...  12.3 us
    pallas_call x1, Pallas kernels, offset_mix(): pl.pallas_call(functools.partial(inner_kernel, taps, count, reach), grid=...  6.19 us
    ppermute x1, starting transfers between devices, body(): before = lax.ppermute(tail, 'off', [(i, i + 1) for i in range(ends)])  4.83 us
    ppermute x1, waiting for transfers between devices, body(): after = lax.ppermute(head, 'off', [(i + 1, i) for i in range(ends)])  4.39 us
    dot_general x1, matrix products, block_filter(): jnp.einsum('...ki,io->...ko', extended, table, precision=lax.Precision.HI...  3.55 us
    unnamed x15, local copies, waits for them, and re-layouts  2.85 us
  transfers between devices with their start and end apart: 2, of which 2 were waited for; matrix products, arithmetic and copies ran while one was open for 0% of the time, Pallas kernels for 5%

profile of v8, /device:TPU:1, one launch (start us, length us, event | category | flops | bytes accessed | tf_op | source)
XLA Modules:
  0.0 114.8 jit_solution(16360329456982804152)
XLA Ops:
  0.0 0.0 copy-start.6
  0.0 1.9 %copy.10 = f32[256,2048]{0,1:T(8,128)S(1)} copy(f32[256,2048]{1,0:T(8,128)} %param.6) | data formatting | bytes 4194304 | tf_op args[0]
  1.9 0.1 fusion.13
  2.1 0.0 copy-done.6
  2.1 0.8 select_reduce_fusion
  2.8 3.6 %fusion = f32[256,16,128]{0,2,1:T(8,128)} fusion(f32[256,15,32]{0,2,1:T(8,128)S(1)} %get-tuple-element.8, f32[256,15,32]{0,2,1:T(8,128)S(1)} %get-tuple-element.7, f32[256,16,128]{0,2,1:T(8,128)S(1)} %bitcast.16, f32[192,128]{1,0:T(8,128)S(1)} %select_reduce_fusion), kind=kOutput, calls=%fused_computation.4 | convolution fusion | flops 1212678144 | bytes 5275648 | tf_op jit(solution)/shard_map/...ki,io->...ko/dot_general | solution.py:33
  6.4 0.0 copy-start.3
  6.4 0.0 copy-start.4
  6.4 0.0 copy-start.5
  6.4 2.0 %copy.11 = f32[256,8,256]{2,0,1:T(8,128)S(1)} copy(f32[256,8,256]{0,2,1:T(8,128)} %bitcast.17) | data formatting | bytes 4194304 | tf_op jit(solution)/shard_map/reshape;reshape | solution.py:151
  8.4 0.0 copy-done.3
  8.4 0.0 copy-done.4
  8.4 0.2 select_reduce_fusion.1
  8.6 0.0 copy-done.5
  8.6 0.1 pad_maximum_fusion
  8.7 55.6 %all_to_all.5 = f32[8,257,256]{2,1,0:T(8,128)S(1)} all-to-all(f32[8,257,256]{2,1,0:T(8,128)S(1)} %pad_maximum_fusion), channel_id=1, replica_groups=mesh['shot'=8,'off'=4] {'shot'}, dimensions={0} | all-to-all | bytes 4210688 | tf_op jit(solution)/shard_map/all_to_all | solution.py:153
  64.3 0.0 copy-start.2
  64.4 1.8 %convert_reduce_fusion = f32[2048]{0:T(1024)S(1)} fusion(s32[2048]{0:T(1024)S(1)} %bitcast.20), kind=kLoop, calls=%fused_computation | loop fusion | flops 12580864 | bytes 16384 | tf_op jit(solution)/shard_map/reduce_sum | solution.py:158
  66.1 0.6 maximum_divide_fusion.scale_ref
  66.7 1.5 %slice.35 = f32[8,256,256]{2,1,0:T(8,128)} slice(f32[8,257,256]{2,1,0:T(8,128)S(1)} %all_to_all.5), slice={[0:8], [0:256], [0:256]} | slice | bytes 4194304 | tf_op jit(solution)/shard_map/slice | solution.py:154
  68.3 0.0 copy-done.2
  68.3 12.3 %shard_map.64 = f32[5120,256]{1,0:T(8,128)} custom-call(s32[2048]{0:T(1024)} %bitcast.21, f32[2048]{0:T(1024)} %maximum_divide_fusion.scale_ref, f32[2048,256]{1,0:T(8,128)} %bitcast.13), custom_call_target="tpu_custom_call" | custom-call | tf_op jit(solution)/shard_map/pallas_call | solution.py:121
  80.6 1.5 %fusion.12 = (f32[768,256]{1,0:T(8,128)S(1)}, f32[768,256]{1,0:T(8,128)S(1)}) fusion(f32[5120,256]{1,0:T(8,128)} %shard_map.64), kind=kLoop, calls=%fused_computation.26 | loop fusion | bytes 3145728 | tf_op jit(solution)/shard_map/slice | solution.py:164
  82.1 4.8 %collective-permute-start = (f32[3,256,256]{2,1,0:T(8,128)S(1)}, f32[3,256,256]{2,1,0:T(8,128)S(1)}, u32[]{:S(2)}, u32[]{:S(2)}) collective-permute-start(f32[3,256,256]{2,1,0:T(8,128)S(1)} %bitcast.19), channel_id=1, source_target_pairs={{0,1},{1,2},{2,3},{4,5},{5,6},{6,7},{8,9},{9,10},{10,11},{12,13},{... | collective-permute-start | bytes 2359304 | tf_op jit(solution)/shard_map/ppermute | solution.py:166
  86.9 1.9 %collective-permute-start.1 = (f32[3,256,256]{2,1,0:T(8,128)S(1)}, f32[3,256,256]{2,1,0:T(8,128)S(1)}, u32[]{:S(2)}, u32[]{:S(2)}) collective-permute-start(f32[3,256,256]{2,1,0:T(8,128)S(1)} %bitcast.18), channel_id=1, source_target_pairs={{1,0},{2,1},{3,2},{5,4},{6,5},{7,6},{9,8},{10,9},{11,10},{13,12},{... | collective-permute-start | bytes 2359304 | tf_op jit(solution)/shard_map/ppermute | solution.py:167
  88.8 6.2 %shard_map.65._ = f32[20,256,256]{2,1,0:T(8,128)} custom-call(f32[7]{0:T(128)} %filter_ref.3, f32[20,256,256]{2,1,0:T(8,128)} %bitcast.11), custom_call_target="tpu_custom_call" | custom-call | tf_op jit(solution)/shard_map/pallas_call | solution.py:76
  95.0 0.8 collective-permute-done.before_ref
  95.8 0.0 copy-start
  95.8 4.4 %collective-permute-done.1.after_ref = f32[3,256,256]{2,1,0:T(8,128)S(1)} collective-permute-done((f32[3,256,256]{2,1,0:T(8,128)S(1)}, f32[3,256,256]{2,1,0:T(8,128)S(1)}, u32[]{:S(2)}, u32[]{:S(2)}) %collective-permute-start.1) | collective-permute-done | bytes 786464 | tf_op jit(solution)/shard_map/ppermute | solution.py:167
  100.2 0.0 copy-done
  100.2 0.0 copy-start.1
  100.2 0.9 copy-done.1
  101.1 13.6 %shard_map.66 = f32[20,256,256]{2,1,0:T(8,128)} custom-call(f32[7]{0:T(128)} %filter_ref.3, f32[3,256,256]{2,1,0:T(8,128)} %copy-done, f32[20,256,256]{2,1,0:T(8,128)} %bitcast.12, f32[3,256,256]{2,1,0:T(8,128)} %copy-done.1, f32[20,256,256]{2,1,0:T(8,128)} %shard_map.65._), custom_call_target="tpu_custom_call", output_to_operand_aliasing={{}: (4, {})} | custom-call | tf_op jit(solution)/shard_map/pallas_call | solution.py:87
  (4 shorter events, 0.0 us)
Async XLA Ops:
  0.0 2.1 %copy-start.6 = (f32[65]{0:T(128)S(1)}, f32[65]{0:T(128)}, u32[]{:S(2)}) copy-start(f32[65]{0:T(128)} %param.11) | copy-start | bytes 784
  6.4 2.0 %copy-start.3 = (s32[256]{0:T(256)S(1)}, s32[256]{0:T(256)}, u32[]{:S(2)}) copy-start(s32[256]{0:T(256)} %param.9) | copy-start | bytes 3076
  6.4 2.0 %copy-start.4 = (s32[256]{0:T(256)S(1)}, s32[256]{0:T(256)}, u32[]{:S(2)}) copy-start(s32[256]{0:T(256)} %param.7) | copy-start | bytes 3076
  6.4 2.2 %copy-start.5 = (s32[256]{0:T(256)S(1)}, s32[256]{0:T(256)}, u32[]{:S(2)}) copy-start(s32[256]{0:T(256)} %param.8) | copy-start | bytes 3076
  64.3 3.9 %copy-start.2 = (s32[8,1,256]{2,1,0:T(1,128)}, s32[8,1,256]{2,1,0:T(1,128)S(1)}, u32[]{:S(2)}) copy-start(s32[8,1,256]{2,1,0:T(1,128)S(1)} %slice_convert_fusion) | copy-start | bytes 24580
  82.1 13.8 %collective-permute-start = (f32[3,256,256]{2,1,0:T(8,128)S(1)}, f32[3,256,256]{2,1,0:T(8,128)S(1)}, u32[]{:S(2)}, u32[]{:S(2)}) collective-permute-start(f32[3,256,256]{2,1,0:T(8,128)S(1)} %bitcast.19), channel_id=1, source_target_pairs={{0,1},{1,2},{2,3},{4,5},{5,6},{6,7},{8,9},{9,10},{10,11},{12,13},{... | collective-permute-start | bytes 2359304 | tf_op jit(solution)/shard_map/ppermute | solution.py:166
  86.9 13.3 %collective-permute-start.1 = (f32[3,256,256]{2,1,0:T(8,128)S(1)}, f32[3,256,256]{2,1,0:T(8,128)S(1)}, u32[]{:S(2)}, u32[]{:S(2)}) collective-permute-start(f32[3,256,256]{2,1,0:T(8,128)S(1)} %bitcast.18), channel_id=1, source_target_pairs={{1,0},{2,1},{3,2},{5,4},{6,5},{7,6},{9,8},{10,9},{11,10},{13,12},{... | collective-permute-start | bytes 2359304 | tf_op jit(solution)/shard_map/ppermute | solution.py:167
  95.8 4.4 %copy-start = (f32[3,256,256]{2,1,0:T(8,128)}, f32[3,256,256]{2,1,0:T(8,128)S(1)}, u32[]{:S(2)}) copy-start(f32[3,256,256]{2,1,0:T(8,128)S(1)} %collective-permute-done.before_ref) | copy-start | bytes 2359300
  100.2 0.9 copy-start.1

commit v9 on v8

--- a/solution.py
+++ b/solution.py
@@ -84,6 +84,7 @@
         out_shape=jax.ShapeDtypeStruct((count, cols, rows), jnp.float32),
     )(filter_off, own)
     shift = count - 2 * reach
+    tile = 256 if rows % 256 == 0 and cols % 256 == 0 else 128
     return pl.pallas_call(
         functools.partial(edge_kernel, taps, count, reach),
         grid=(rows // tile, cols // tile, 2 * reach),

time: 115 us -> 107 us (0.930)
  Pallas kernels: 32.2 us -> 24.4 us
    pallas_call x1, Pallas kernels: 13.6 us -> 5.92 us  [offset_mix(): pl.pallas_call(functools.partial(edge_kernel, taps, count, reach), grid=(...]
  transfers between devices with their start and end apart: 2 -> 2, of which waited for: 2 -> 2; matrix products, arithmetic and copies ran while one was open for 0% -> 0% of each run, Pallas kernels for 5% -> 6%
where the time goes in v9:
time: 107 us
  blocking collectives  55.6 us (52%)
  Pallas kernels  24.4 us (23%)
  local copies, waits for them, and re-layouts  7.91 us (7%)
  starting transfers between devices  6.75 us (6%)
  waiting for transfers between devices  5.18 us (5%)
  matrix products  3.55 us (3%)
  other arithmetic  3.49 us (3%)
    all_to_all x1, blocking collectives, body(): received = lax.all_to_all(outgoing, 'shot', 0, 0, tiled=True)  55.6 us
    pallas_call x1, Pallas kernels, stack_rows(): pl.pallas_call(functools.partial(scatter_kernel, count), in_specs=[pl.Blo...  12.3 us
    pallas_call x1, Pallas kernels, offset_mix(): pl.pallas_call(functools.partial(inner_kernel, taps, count, reach), grid=...  6.19 us
    pallas_call x1, Pallas kernels, offset_mix(): pl.pallas_call(functools.partial(edge_kernel, taps, count, reach), grid=(...  5.92 us
    ppermute x1, starting transfers between devices, body(): before = lax.ppermute(tail, 'off', [(i, i + 1) for i in range(ends)])  4.83 us
    ppermute x1, waiting for transfers between devices, body(): after = lax.ppermute(head, 'off', [(i + 1, i) for i in range(ends)])  4.39 us
    dot_general x1, matrix products, block_filter(): jnp.einsum('...ki,io->...ko', extended, table, precision=lax.Precision.HI...  3.55 us
    unnamed x15, local copies, waits for them, and re-layouts  2.85 us
  transfers between devices with their start and end apart: 2, of which 2 were waited for; matrix products, arithmetic and copies ran while one was open for 0% of the time, Pallas kernels for 6%

profile of v9, /device:TPU:1, one launch (start us, length us, event | category | flops | bytes accessed | tf_op | source)
XLA Modules:
  0.0 107.0 jit_solution(9839883657812065552)
XLA Ops:
  0.0 0.0 copy-start.6
  0.0 1.9 %copy.10 = f32[256,2048]{0,1:T(8,128)S(1)} copy(f32[256,2048]{1,0:T(8,128)} %param.6) | data formatting | bytes 4194304 | tf_op args[0]
  1.9 0.1 fusion.13
  2.1 0.0 copy-done.6
  2.1 0.8 select_reduce_fusion
  2.8 3.6 %fusion = f32[256,16,128]{0,2,1:T(8,128)} fusion(f32[256,15,32]{0,2,1:T(8,128)S(1)} %get-tuple-element.8, f32[256,15,32]{0,2,1:T(8,128)S(1)} %get-tuple-element.7, f32[256,16,128]{0,2,1:T(8,128)S(1)} %bitcast.16, f32[192,128]{1,0:T(8,128)S(1)} %select_reduce_fusion), kind=kOutput, calls=%fused_computation.4 | convolution fusion | flops 1212678144 | bytes 5275648 | tf_op jit(solution)/shard_map/...ki,io->...ko/dot_general | solution.py:33
  6.4 0.0 copy-start.3
  6.4 0.0 copy-start.4
  6.4 0.0 copy-start.5
  6.4 2.0 %copy.11 = f32[256,8,256]{2,0,1:T(8,128)S(1)} copy(f32[256,8,256]{0,2,1:T(8,128)} %bitcast.17) | data formatting | bytes 4194304 | tf_op jit(solution)/shard_map/reshape;reshape | solution.py:152
  8.4 0.0 copy-done.3
  8.4 0.0 copy-done.4
  8.4 0.2 select_reduce_fusion.1
  8.6 0.0 copy-done.5
  8.6 0.1 pad_maximum_fusion
  8.7 55.6 %all_to_all.5 = f32[8,257,256]{2,1,0:T(8,128)S(1)} all-to-all(f32[8,257,256]{2,1,0:T(8,128)S(1)} %pad_maximum_fusion), channel_id=1, replica_groups=mesh['shot'=8,'off'=4] {'shot'}, dimensions={0} | all-to-all | bytes 4210688 | tf_op jit(solution)/shard_map/all_to_all | solution.py:154
  64.3 0.0 copy-start.2
  64.4 1.8 %convert_reduce_fusion = f32[2048]{0:T(1024)S(1)} fusion(s32[2048]{0:T(1024)S(1)} %bitcast.20), kind=kLoop, calls=%fused_computation | loop fusion | flops 12580864 | bytes 16384 | tf_op jit(solution)/shard_map/reduce_sum | solution.py:159
  66.1 0.6 maximum_divide_fusion.scale_ref
  66.7 1.5 %slice.35 = f32[8,256,256]{2,1,0:T(8,128)} slice(f32[8,257,256]{2,1,0:T(8,128)S(1)} %all_to_all.5), slice={[0:8], [0:256], [0:256]} | slice | bytes 4194304 | tf_op jit(solution)/shard_map/slice | solution.py:155
  68.3 0.0 copy-done.2
  68.3 12.3 %shard_map.64 = f32[5120,256]{1,0:T(8,128)} custom-call(s32[2048]{0:T(1024)} %bitcast.21, f32[2048]{0:T(1024)} %maximum_divide_fusion.scale_ref, f32[2048,256]{1,0:T(8,128)} %bitcast.13), custom_call_target="tpu_custom_call" | custom-call | tf_op jit(solution)/shard_map/pallas_call | solution.py:122
  80.6 1.5 %fusion.12 = (f32[768,256]{1,0:T(8,128)S(1)}, f32[768,256]{1,0:T(8,128)S(1)}) fusion(f32[5120,256]{1,0:T(8,128)} %shard_map.64), kind=kLoop, calls=%fused_computation.26 | loop fusion | bytes 3145728 | tf_op jit(solution)/shard_map/slice | solution.py:165
  82.1 4.8 %collective-permute-start = (f32[3,256,256]{2,1,0:T(8,128)S(1)}, f32[3,256,256]{2,1,0:T(8,128)S(1)}, u32[]{:S(2)}, u32[]{:S(2)}) collective-permute-start(f32[3,256,256]{2,1,0:T(8,128)S(1)} %bitcast.19), channel_id=1, source_target_pairs={{0,1},{1,2},{2,3},{4,5},{5,6},{6,7},{8,9},{9,10},{10,11},{12,13},{... | collective-permute-start | bytes 2359304 | tf_op jit(solution)/shard_map/ppermute | solution.py:167
  86.9 1.9 %collective-permute-start.1 = (f32[3,256,256]{2,1,0:T(8,128)S(1)}, f32[3,256,256]{2,1,0:T(8,128)S(1)}, u32[]{:S(2)}, u32[]{:S(2)}) collective-permute-start(f32[3,256,256]{2,1,0:T(8,128)S(1)} %bitcast.18), channel_id=1, source_target_pairs={{1,0},{2,1},{3,2},{5,4},{6,5},{7,6},{9,8},{10,9},{11,10},{13,12},{... | collective-permute-start | bytes 2359304 | tf_op jit(solution)/shard_map/ppermute | solution.py:168
  88.8 6.2 %shard_map.65._ = f32[20,256,256]{2,1,0:T(8,128)} custom-call(f32[7]{0:T(128)} %filter_ref.3, f32[20,256,256]{2,1,0:T(8,128)} %bitcast.11), custom_call_target="tpu_custom_call" | custom-call | tf_op jit(solution)/shard_map/pallas_call | solution.py:76
  95.0 0.8 collective-permute-done.before_ref
  95.8 0.0 copy-start
  95.8 4.4 %collective-permute-done.1.after_ref = f32[3,256,256]{2,1,0:T(8,128)S(1)} collective-permute-done((f32[3,256,256]{2,1,0:T(8,128)S(1)}, f32[3,256,256]{2,1,0:T(8,128)S(1)}, u32[]{:S(2)}, u32[]{:S(2)}) %collective-permute-start.1) | collective-permute-done | bytes 786464 | tf_op jit(solution)/shard_map/ppermute | solution.py:168
  100.2 0.0 copy-done
  100.2 0.0 copy-start.1
  100.2 0.9 copy-done.1
  101.1 5.9 %shard_map.66 = f32[20,256,256]{2,1,0:T(8,128)} custom-call(f32[7]{0:T(128)} %filter_ref.3, f32[3,256,256]{2,1,0:T(8,128)} %copy-done, f32[20,256,256]{2,1,0:T(8,128)} %bitcast.12, f32[3,256,256]{2,1,0:T(8,128)} %copy-done.1, f32[20,256,256]{2,1,0:T(8,128)} %shard_map.65._), custom_call_target="tpu_custom_call", output_to_operand_aliasing={{}: (4, {})} | custom-call | tf_op jit(solution)/shard_map/pallas_call | solution.py:88
  (4 shorter events, 0.0 us)
Async XLA Ops:
  0.0 2.1 %copy-start.6 = (f32[65]{0:T(128)S(1)}, f32[65]{0:T(128)}, u32[]{:S(2)}) copy-start(f32[65]{0:T(128)} %param.11) | copy-start | bytes 784
  6.4 2.0 %copy-start.3 = (s32[256]{0:T(256)S(1)}, s32[256]{0:T(256)}, u32[]{:S(2)}) copy-start(s32[256]{0:T(256)} %param.9) | copy-start | bytes 3076
  6.4 2.0 %copy-start.4 = (s32[256]{0:T(256)S(1)}, s32[256]{0:T(256)}, u32[]{:S(2)}) copy-start(s32[256]{0:T(256)} %param.7) | copy-start | bytes 3076
  6.4 2.2 %copy-start.5 = (s32[256]{0:T(256)S(1)}, s32[256]{0:T(256)}, u32[]{:S(2)}) copy-start(s32[256]{0:T(256)} %param.8) | copy-start | bytes 3076
  64.3 3.9 %copy-start.2 = (s32[8,1,256]{2,1,0:T(1,128)}, s32[8,1,256]{2,1,0:T(1,128)S(1)}, u32[]{:S(2)}) copy-start(s32[8,1,256]{2,1,0:T(1,128)S(1)} %slice_convert_fusion) | copy-start | bytes 24580
  82.1 13.8 %collective-permute-start = (f32[3,256,256]{2,1,0:T(8,128)S(1)}, f32[3,256,256]{2,1,0:T(8,128)S(1)}, u32[]{:S(2)}, u32[]{:S(2)}) collective-permute-start(f32[3,256,256]{2,1,0:T(8,128)S(1)} %bitcast.19), channel_id=1, source_target_pairs={{0,1},{1,2},{2,3},{4,5},{5,6},{6,7},{8,9},{9,10},{10,11},{12,13},{... | collective-permute-start | bytes 2359304 | tf_op jit(solution)/shard_map/ppermute | solution.py:167
  86.9 13.3 %collective-permute-start.1 = (f32[3,256,256]{2,1,0:T(8,128)S(1)}, f32[3,256,256]{2,1,0:T(8,128)S(1)}, u32[]{:S(2)}, u32[]{:S(2)}) collective-permute-start(f32[3,256,256]{2,1,0:T(8,128)S(1)} %bitcast.18), channel_id=1, source_target_pairs={{1,0},{2,1},{3,2},{5,4},{6,5},{7,6},{9,8},{10,9},{11,10},{13,12},{... | collective-permute-start | bytes 2359304 | tf_op jit(solution)/shard_map/ppermute | solution.py:168
  95.8 4.4 %copy-start = (f32[3,256,256]{2,1,0:T(8,128)}, f32[3,256,256]{2,1,0:T(8,128)S(1)}, u32[]{:S(2)}) copy-start(f32[3,256,256]{2,1,0:T(8,128)S(1)} %collective-permute-done.before_ref) | copy-start | bytes 2359300
  100.2 0.9 copy-start.1

commit v10 on v9

--- a/solution.py
+++ b/solution.py
@@ -101,12 +101,14 @@
     )(filter_off, before, own, after, inner)
 
 
-def scatter_kernel(count, cell_ref, scale_ref, rows_ref, out_ref):
+def scatter_kernel(count, tr_dev, cell_ref, scale_ref, rows_ref, out_ref):
     out_ref[...] = jnp.zeros(out_ref.shape, jnp.float32)
 
     def step(i, carry):
         start = pl.multiple_of(i * 8, 8)
-        tile = rows_ref[pl.ds(start, 8), :]
+        src = start // tr_dev
+        local = pl.multiple_of(start - src * tr_dev, 8)
+        tile = rows_ref[src, pl.ds(local, 8), :]
         for k in range(8):
             x = cell_ref[start + k]
             out_ref[pl.ds(x, 1), :] += tile[k : k + 1, :] * scale_ref[start + k]
@@ -115,12 +117,15 @@
     lax.fori_loop(0, count // 8, step, 0)
 
 
-def stack_rows(rows, cells, scale, segments):
-    count, width = rows.shape
-    if width % 128 or count % 8:
+def stack_rows(received, cells, scale, segments):
+    shots, _, width = received.shape
+    count = cells.shape[0]
+    tr_dev = count // shots
+    if width % 128 or tr_dev % 8:
+        rows = received[:, :tr_dev].reshape(count, width)
         return jax.ops.segment_sum(rows * scale[:, None], cells, num_segments=segments)
     return pl.pallas_call(
-        functools.partial(scatter_kernel, count),
+        functools.partial(scatter_kernel, count, tr_dev),
         in_specs=[
             pl.BlockSpec(memory_space=pltpu.SMEM),
             pl.BlockSpec(memory_space=pltpu.SMEM),
@@ -128,7 +133,7 @@
         ],
         out_specs=pl.BlockSpec(memory_space=pltpu.VMEM),
         out_shape=jax.ShapeDtypeStruct((segments, width), jnp.float32),
-    )(cells, scale, rows)
+    )(cells, scale, received)
 
 
 def body(traces, cmp_bin, offset_class, bin_rank, filter_off, filter_time):
@@ -152,13 +157,12 @@
     outgoing = jnp.transpose(filtered.reshape(tr_dev, shots, window), (1, 0, 2))
     outgoing = jnp.concatenate([outgoing, labels], axis=1)
     received = lax.all_to_all(outgoing, "shot", 0, 0, tiled=True)
-    rows = received[:, :tr_dev].reshape(shots * tr_dev, window)
     cells = received[:, tr_dev:].reshape(shots, label_rows * window)[:, :tr_dev]
     cells = cells.reshape(shots * tr_dev).astype(jnp.int32)
 
     fold = jnp.sum((cells[:, None] == cells[None, :]).astype(jnp.float32), axis=1)
     scale = 1.0 / jnp.maximum(fold, 1.0)
-    stacked = stack_rows(rows, cells, scale, off_dev * bin_count)
+    stacked = stack_rows(received, cells, scale, off_dev * bin_count)
     stacked = stacked.reshape(off_dev, bin_count, window)
 
     ends = off_count - 1

time: 107 us -> 107 us (level)
  local copies, waits for them, and re-layouts: 7.91 us -> 6.38 us
  Pallas kernels: 24.4 us -> 25.9 us
    slice x1 -> x0, local copies, waits for them, and re-layouts: 1.53 us -> none  [body(): rows = received[:, :tr_dev].reshape(shots * tr_dev, window)]
    pallas_call x1, Pallas kernels: 12.3 us -> 13.8 us  [stack_rows(): pl.pallas_call(functools.partial(scatter_kernel, count, tr_dev), in_specs...]
    unnamed x15 -> x17, local copies, waits for them, and re-layouts: 2.85 us -> 2.85 us
where the time goes in v10:
time: 107 us
  blocking collectives  55.6 us (52%)
  Pallas kernels  25.9 us (24%)
  starting transfers between devices  6.75 us (6%)
  local copies, waits for them, and re-layouts  6.38 us (6%)
  waiting for transfers between devices  5.18 us (5%)
  matrix products  3.55 us (3%)
  other arithmetic  3.49 us (3%)
    all_to_all x1, blocking collectives, body(): received = lax.all_to_all(outgoing, 'shot', 0, 0, tiled=True)  55.6 us
    pallas_call x1, Pallas kernels, stack_rows(): pl.pallas_call(functools.partial(scatter_kernel, count, tr_dev), in_specs...  13.8 us
    pallas_call x1, Pallas kernels, offset_mix(): pl.pallas_call(functools.partial(inner_kernel, taps, count, reach), grid=...  6.19 us
    pallas_call x1, Pallas kernels, offset_mix(): pl.pallas_call(functools.partial(edge_kernel, taps, count, reach), grid=(...  5.92 us
    ppermute x1, starting transfers between devices, body(): before = lax.ppermute(tail, 'off', [(i, i + 1) for i in range(ends)])  4.83 us
    ppermute x1, waiting for transfers between devices, body(): after = lax.ppermute(head, 'off', [(i + 1, i) for i in range(ends)])  4.39 us
    dot_general x1, matrix products, block_filter(): jnp.einsum('...ki,io->...ko', extended, table, precision=lax.Precision.HI...  3.55 us
    unnamed x17, local copies, waits for them, and re-layouts  2.85 us
  transfers between devices with their start and end apart: 2, of which 2 were waited for; matrix products, arithmetic and copies ran while one was open for 0% of the time, Pallas kernels for 6%

profile of v10, /device:TPU:1, one launch (start us, length us, event | category | flops | bytes accessed | tf_op | source)
XLA Modules:
  0.0 107.0 jit_solution(1154328021400038836)
XLA Ops:
  0.0 0.0 copy-start.7
  0.0 1.9 %copy.11 = f32[256,2048]{0,1:T(8,128)S(1)} copy(f32[256,2048]{1,0:T(8,128)} %param.6) | data formatting | bytes 4194304 | tf_op args[0]
  1.9 0.1 fusion.13
  2.1 0.0 copy-done.7
  2.1 0.8 select_reduce_fusion
  2.8 3.6 %fusion = f32[256,16,128]{0,2,1:T(8,128)} fusion(f32[256,15,32]{0,2,1:T(8,128)S(1)} %get-tuple-element.8, f32[256,15,32]{0,2,1:T(8,128)S(1)} %get-tuple-element.7, f32[256,16,128]{0,2,1:T(8,128)S(1)} %bitcast.14, f32[192,128]{1,0:T(8,128)S(1)} %select_reduce_fusion), kind=kOutput, calls=%fused_computation.4 | convolution fusion | flops 1212678144 | bytes 5275648 | tf_op jit(solution)/shard_map/...ki,io->...ko/dot_general | solution.py:33
  6.4 0.0 copy-start.4
  6.4 0.0 copy-start.5
  6.4 0.0 copy-start.6
  6.4 2.0 %copy.12 = f32[256,8,256]{2,0,1:T(8,128)S(1)} copy(f32[256,8,256]{0,2,1:T(8,128)} %bitcast.15) | data formatting | bytes 4194304 | tf_op jit(solution)/shard_map/reshape;reshape | solution.py:157
  8.4 0.0 copy-done.4
  8.4 0.0 copy-done.5
  8.4 0.2 select_reduce_fusion.1
  8.6 0.0 copy-done.6
  8.6 0.1 pad_maximum_fusion
  8.7 55.6 %all_to_all.5.rows_ref = f32[8,257,256]{2,1,0:T(8,128)S(1)} all-to-all(f32[8,257,256]{2,1,0:T(8,128)S(1)} %pad_maximum_fusion), channel_id=1, replica_groups=mesh['shot'=8,'off'=4] {'shot'}, dimensions={0} | all-to-all | bytes 4210688 | tf_op jit(solution)/shard_map/all_to_all | solution.py:159
  64.3 0.0 copy-start
  64.3 0.0 copy-start.3
  64.4 1.8 %convert_reduce_fusion = f32[2048]{0:T(1024)S(1)} fusion(s32[2048]{0:T(1024)S(1)} %bitcast.18), kind=kLoop, calls=%fused_computation | loop fusion | flops 12580864 | bytes 16384 | tf_op jit(solution)/shard_map/reduce_sum | solution.py:163
  66.1 0.6 maximum_divide_fusion.scale_ref
  66.7 0.0 copy-done
  66.7 0.0 copy-done.3
  66.7 13.8 %shard_map.64 = f32[5120,256]{1,0:T(8,128)} custom-call(s32[2048]{0:T(1024)} %bitcast.19, f32[2048]{0:T(1024)} %maximum_divide_fusion.scale_ref, f32[8,257,256]{2,1,0:T(8,128)} %copy-done), custom_call_target="tpu_custom_call" | custom-call | tf_op jit(solution)/shard_map/pallas_call | solution.py:127
  80.6 1.5 %fusion.12 = (f32[768,256]{1,0:T(8,128)S(1)}, f32[768,256]{1,0:T(8,128)S(1)}) fusion(f32[5120,256]{1,0:T(8,128)} %shard_map.64), kind=kLoop, calls=%fused_computation.26 | loop fusion | bytes 3145728 | tf_op jit(solution)/shard_map/slice | solution.py:169
  82.0 4.8 %collective-permute-start = (f32[3,256,256]{2,1,0:T(8,128)S(1)}, f32[3,256,256]{2,1,0:T(8,128)S(1)}, u32[]{:S(2)}, u32[]{:S(2)}) collective-permute-start(f32[3,256,256]{2,1,0:T(8,128)S(1)} %bitcast.17), channel_id=1, source_target_pairs={{0,1},{1,2},{2,3},{4,5},{5,6},{6,7},{8,9},{9,10},{10,11},{12,13},{... | collective-permute-start | bytes 2359304 | tf_op jit(solution)/shard_map/ppermute | solution.py:171
  86.9 1.9 %collective-permute-start.1 = (f32[3,256,256]{2,1,0:T(8,128)S(1)}, f32[3,256,256]{2,1,0:T(8,128)S(1)}, u32[]{:S(2)}, u32[]{:S(2)}) collective-permute-start(f32[3,256,256]{2,1,0:T(8,128)S(1)} %bitcast.16), channel_id=1, source_target_pairs={{1,0},{2,1},{3,2},{5,4},{6,5},{7,6},{9,8},{10,9},{11,10},{13,12},{... | collective-permute-start | bytes 2359304 | tf_op jit(solution)/shard_map/ppermute | solution.py:172
  88.8 6.2 %shard_map.65._ = f32[20,256,256]{2,1,0:T(8,128)} custom-call(f32[7]{0:T(128)} %filter_ref.3, f32[20,256,256]{2,1,0:T(8,128)} %bitcast.10), custom_call_target="tpu_custom_call" | custom-call | tf_op jit(solution)/shard_map/pallas_call | solution.py:76
  95.0 0.8 collective-permute-done.before_ref
  95.8 0.0 copy-start.1
  95.8 4.4 %collective-permute-done.1.after_ref = f32[3,256,256]{2,1,0:T(8,128)S(1)} collective-permute-done((f32[3,256,256]{2,1,0:T(8,128)S(1)}, f32[3,256,256]{2,1,0:T(8,128)S(1)}, u32[]{:S(2)}, u32[]{:S(2)}) %collective-permute-start.1) | collective-permute-done | bytes 786464 | tf_op jit(solution)/shard_map/ppermute | solution.py:172
  100.2 0.0 copy-done.1
  100.2 0.0 copy-start.2
  100.2 0.9 copy-done.2
  101.1 5.9 %shard_map.66 = f32[20,256,256]{2,1,0:T(8,128)} custom-call(f32[7]{0:T(128)} %filter_ref.3, f32[3,256,256]{2,1,0:T(8,128)} %copy-done.1, f32[20,256,256]{2,1,0:T(8,128)} %bitcast.11, f32[3,256,256]{2,1,0:T(8,128)} %copy-done.2, f32[20,256,256]{2,1,0:T(8,128)} %shard_map.65._), custom_call_target="tpu_custom_call", output_to_operand_aliasing={{}: (4, {})} | custom-call | tf_op jit(solution)/shard_map/pallas_call | solution.py:88
  (4 shorter events, 0.0 us)
Async XLA Ops:
  0.0 2.1 %copy-start.7 = (f32[65]{0:T(128)S(1)}, f32[65]{0:T(128)}, u32[]{:S(2)}) copy-start(f32[65]{0:T(128)} %param.11) | copy-start | bytes 784
  6.4 2.0 %copy-start.4 = (s32[256]{0:T(256)S(1)}, s32[256]{0:T(256)}, u32[]{:S(2)}) copy-start(s32[256]{0:T(256)} %param.9) | copy-start | bytes 3076
  6.4 2.0 %copy-start.5 = (s32[256]{0:T(256)S(1)}, s32[256]{0:T(256)}, u32[]{:S(2)}) copy-start(s32[256]{0:T(256)} %param.7) | copy-start | bytes 3076
  6.4 2.2 %copy-start.6 = (s32[256]{0:T(256)S(1)}, s32[256]{0:T(256)}, u32[]{:S(2)}) copy-start(s32[256]{0:T(256)} %param.8) | copy-start | bytes 3076
  64.3 2.4 %copy-start = (f32[8,257,256]{2,1,0:T(8,128)}, f32[8,257,256]{2,1,0:T(8,128)S(1)}, u32[]{:S(2)}) copy-start(f32[8,257,256]{2,1,0:T(8,128)S(1)} %all_to_all.5.rows_ref) | copy-start | bytes 6316036
  64.3 2.4 %copy-start.3 = (s32[8,1,256]{2,1,0:T(1,128)}, s32[8,1,256]{2,1,0:T(1,128)S(1)}, u32[]{:S(2)}) copy-start(s32[8,1,256]{2,1,0:T(1,128)S(1)} %slice_convert_fusion) | copy-start | bytes 24580
  82.0 13.8 %collective-permute-start = (f32[3,256,256]{2,1,0:T(8,128)S(1)}, f32[3,256,256]{2,1,0:T(8,128)S(1)}, u32[]{:S(2)}, u32[]{:S(2)}) collective-permute-start(f32[3,256,256]{2,1,0:T(8,128)S(1)} %bitcast.17), channel_id=1, source_target_pairs={{0,1},{1,2},{2,3},{4,5},{5,6},{6,7},{8,9},{9,10},{10,11},{12,13},{... | collective-permute-start | bytes 2359304 | tf_op jit(solution)/shard_map/ppermute | solution.py:171
  86.9 13.3 %collective-permute-start.1 = (f32[3,256,256]{2,1,0:T(8,128)S(1)}, f32[3,256,256]{2,1,0:T(8,128)S(1)}, u32[]{:S(2)}, u32[]{:S(2)}) collective-permute-start(f32[3,256,256]{2,1,0:T(8,128)S(1)} %bitcast.16), channel_id=1, source_target_pairs={{1,0},{2,1},{3,2},{5,4},{6,5},{7,6},{9,8},{10,9},{11,10},{13,12},{... | collective-permute-start | bytes 2359304 | tf_op jit(solution)/shard_map/ppermute | solution.py:172
  95.8 4.4 %copy-start.1 = (f32[3,256,256]{2,1,0:T(8,128)}, f32[3,256,256]{2,1,0:T(8,128)S(1)}, u32[]{:S(2)}) copy-start(f32[3,256,256]{2,1,0:T(8,128)S(1)} %collective-permute-done.before_ref) | copy-start | bytes 2359300
  100.2 0.9 copy-start.2
